TPU v7x, 512 devices: a whole 4x8x8 slice. The times are simulated.
512 devices in a mesh: leaf: 128 (over y, z, core), sub: 4 (over x).
Axes of the slice: x: 4, y: 8, z: 8, core: 2. Of those that a mesh axis runs over, the one named last changes fastest.
Arguments:
- probes: bfloat16 [32, 524288], P(None, ('leaf', 'sub')), may hold values from -6 to 6
- row_basis: bfloat16 [2048, 64, 256], P(('leaf', 'sub')), may hold values from -0.375 to 0.375
- col_basis: bfloat16 [2048, 64, 256], P(('leaf', 'sub')), may hold values from -0.75 to 0.75
- near_blocks: bfloat16 [2048, 5, 256, 256], P(('leaf', 'sub')), may hold values from -0.21875 to 0.21875
- near_cols: int32 [2048, 5], P(('leaf', 'sub')), may hold values from -1 to 2047, as said below
- far_leaf: int32 [2048, 4], P(('leaf', 'sub')), may hold values from -1 to 2047, as said below
- far_pair: int32 [1024, 4], P(('leaf', 'sub')), may hold values from -1 to 1023, as said below
- far_top: int32 [1020, 4], replicated, may hold values from -1 to 511, as said below
- row_transfer: float32 [9, 2, 64, 64], replicated, may hold values from -0.5 to 0.5
- col_transfer: float32 [9, 2, 64, 64], replicated, may hold values from -0.75 to 0.75
- coupling: float32 [10, 6, 64, 64], replicated, may hold values from -0.4375 to 0.4375
Outputs:
- result: float32 [32, 524288], P(None, ('leaf', 'sub'))
Inputs may be any that keep to these rules, and one draw needn't show every extreme that they name: `near_cols`: slot j of leaf s holds s + j - 2 or -1; slot 2 always holds s. `far_leaf`: each entry of the row of box t is -1 or a child of a box beside t's parent, never t itself; a row's entries are distinct. `far_pair`: each entry of the row of box t is -1 or a child of a box beside t's parent, never t itself; a row's entries are distinct. `far_top`: rows of level 2 first, then level 3 and so on, boxes in order; entries are box numbers within their level, -1 or a child of a box beside the row box's parent, never the box itself, distinct within a row.
All inputs are finite; a program needn't handle non-finite values.
Results may differ from a plain program's by a relative error of at most 0.0028.
Values sent between devices are 32-bit elements; how exact they have to be, the bound alone decides.
No kernel may reach another device: no remote copies, remote signals or barrier semaphores. Data moves between devices by JAX's collectives and lax.ppermute only.
A program may use at most 128 MiB of HBM per device.

v0:
```python
import jax
import jax.numpy as jnp
from jax import lax
from jax.sharding import Mesh
from jax.sharding import PartitionSpec as P

highest = lax.Precision.HIGHEST
ALL = ("yz", "core", "sub")
GROUP = ("core", "sub")


def padded(shard, axis, width):
    devices, length = (lax.axis_size(axis), shard.shape[0])
    up = [(i, i + 1) for i in range(devices - 1)]
    down = [(j, i) for i, j in up]
    before = lax.ppermute(shard[length - width :], axis, up)
    after = lax.ppermute(shard[:width], axis, down)
    return jnp.concatenate([before, shard, after], axis=0)


def halve(coefficients, transfer):
    paired = coefficients.reshape(
        coefficients.shape[0] // 2, 2, coefficients.shape[1], coefficients.shape[2]
    )
    return jnp.einsum("bjkr,jrs->bks", paired, transfer, precision=highest)


def window_coupling(windows, bases, rows, odd, level_coupling):
    picks = (0, 1, 4, 5)
    stacked = jnp.concatenate([windows[:, w] for w in picks], axis=-1)
    hits = [
        jnp.any((rows == (bases + w)[:, None]) & (rows >= 0), axis=1) for w in picks
    ]
    even_cls = (1, 2, 4, 5)
    odd_cls = (0, 1, 3, 4)
    mats = []
    for i in range(4):
        chosen = jnp.where(
            odd[:, None, None], level_coupling[odd_cls[i]], level_coupling[even_cls[i]]
        )
        mats.append(jnp.where(hits[i][:, None, None], chosen, 0.0))
    matrix = jnp.concatenate(mats, axis=1)
    return jnp.einsum("bkr,brs->bks", stacked, matrix, precision=highest)


def one_box(level_array, offset, box, row, level_coupling):
    base = 2 * (box >> 1) - 2
    win = lax.dynamic_slice_in_dim(level_array, base - offset, 6, axis=0)
    return window_coupling(
        win[None], jnp.reshape(base, (1,)), row[None], jnp.reshape(box & 1, (1,)) == 1,
        level_coupling,
    )[0]


def local(
    probes,
    row_basis,
    col_basis,
    near_blocks,
    near_cols,
    far_leaf,
    far_pair,
    far_top,
    row_transfer,
    col_transfer,
    coupling,
):
    leaves, basis_rank, leaf_width = row_basis.shape
    probe_count = probes.shape[0]
    near_reach = near_cols.shape[1] // 2
    levels_total = coupling.shape[0]
    devices = lax.axis_size(ALL)
    device = lax.axis_index(ALL)
    group_size = lax.axis_size(GROUP)
    in_group = lax.axis_index(GROUP)
    group = lax.axis_index("yz")
    groups = lax.axis_size("yz")
    all_leaves = devices * leaves
    first_leaf = device * leaves
    points = probes.reshape(probe_count, leaves, leaf_width)

    a0 = jnp.einsum("klp,lrp->lkr", points, row_basis, preferred_element_type=jnp.float32)
    a1 = halve(a0, row_transfer[0])
    a2 = halve(a1, row_transfer[1])

    grp = lax.all_gather(a2[0], GROUP, axis=0, tiled=False)
    up_levels = [grp]
    for height in range(2, 5):
        up_levels.append(halve(up_levels[-1], row_transfer[height]))
    own5 = up_levels[-1]
    top = [lax.all_gather(own5[0], "yz", axis=0, tiled=False)]
    for height in range(5, levels_total - 1):
        top.append(halve(top[-1], row_transfer[height]))

    ext = [padded(grp, "yz", group_size)]
    for height in range(2, 4):
        ext.append(halve(ext[-1], row_transfer[height]))

    products = jnp.einsum("klp,ljpq->ljkq", points, near_blocks, preferred_element_type=jnp.float32)
    span_width = leaves + 2 * near_reach
    targets = near_cols - (first_leaf - near_reach)
    places = jnp.arange(span_width, dtype=jnp.int32)
    scatter_table = (
        (targets[:, :, None] == places[None, None, :]) & (near_cols >= 0)[:, :, None]
    ).astype(jnp.float32)
    spread = jnp.einsum("lje,ljkq->ekq", scatter_table, products, precision=highest)
    rims = jnp.concatenate([spread[:near_reach], spread[span_width - near_reach :]], axis=0)
    rim_ext = padded(rims, ALL, near_reach)
    own_near = spread[near_reach : near_reach + leaves]
    own_near = own_near.at[:near_reach].add(rim_ext[:near_reach])
    own_near = own_near.at[leaves - near_reach :].add(rim_ext[3 * near_reach :])

    packed = jnp.concatenate([a0, a1], axis=0)
    pack_ext = padded(packed, ALL, packed.shape[0])
    rows_pack = packed.shape[0]
    ext0 = jnp.concatenate(
        [pack_ext[:leaves], a0, pack_ext[rows_pack + rows_pack : rows_pack * 2 + leaves]], axis=0
    )
    ext1 = jnp.concatenate(
        [pack_ext[leaves:rows_pack], a1, pack_ext[rows_pack * 2 + leaves :]], axis=0
    )

    starts = {}
    running = 0
    for height in range(2, levels_total):
        starts[height] = running
        running = running + (all_leaves >> height)

    def top_row(height, box):
        return lax.dynamic_index_in_dim(far_top, starts[height] + box, 0, keepdims=False)

    g = {}
    for height in range(5, levels_total):
        arr = top[height - 5]
        arr = jnp.pad(arr, ((2, 2), (0, 0), (0, 0)))
        box = group >> (height - 5)
        g[height] = one_box(arr, -2, box, top_row(height, box), coupling[height])
    for height in range(2, 5):
        arr = ext[height - 2]
        box = device >> (height - 2)
        offset = (group - 1) * (group_size >> (height - 2))
        g[height] = one_box(arr, offset, box, top_row(height, box), coupling[height])

    expansion = g[levels_total - 1]
    for height in range(levels_total - 2, 1, -1):
        box = device >> (height - 2)
        matrix = lax.dynamic_index_in_dim(col_transfer[height], box & 1, 0, keepdims=False)
        expansion = g[height] + jnp.dot(expansion, matrix, precision=highest)

    odd1 = jnp.array([False, True])
    bases1 = jnp.full((2,), 2 * device - 2, jnp.int32)
    win1 = jnp.stack([ext1[0:6], ext1[0:6]], axis=0)
    g1 = window_coupling(win1, bases1, far_pair, odd1, coupling[1])
    b1 = jnp.einsum("kr,jrs->jks", expansion, col_transfer[1], precision=highest) + g1

    odd0 = jnp.array([False, True, False, True])
    local_starts = (2, 2, 4, 4)
    bases0 = first_leaf + jnp.array([0, 0, 2, 2], jnp.int32) - 2
    win0 = jnp.stack([ext0[s : s + 6] for s in local_starts], axis=0)
    g0 = window_coupling(win0, bases0, far_leaf, odd0, coupling[0])
    pushed = jnp.einsum("jkr,crs->jcks", b1, col_transfer[0], precision=highest)
    b0 = pushed.reshape(leaves, probe_count, basis_rank) + g0

    far_field = jnp.einsum(
        "lkr,lrp->klp",
        b0.astype(jnp.bfloat16),
        col_basis,
        preferred_element_type=jnp.float32,
    )
    own_near_t = jnp.transpose(own_near, (1, 0, 2))
    return (far_field + own_near_t).reshape(probe_count, leaves * leaf_width)


def solution(mesh):
    leaf_count, sub_count = mesh.devices.shape
    fine = Mesh(mesh.devices.reshape(leaf_count // 2, 2, sub_count), ALL)
    in_specs = (
        P(None, ALL),
        P(ALL, None, None),
        P(ALL, None, None),
        P(ALL, None, None, None),
        P(ALL, None),
        P(ALL, None),
        P(ALL, None),
        P(),
        P(),
        P(),
        P(),
    )
    out_specs = P(None, ALL)
    return jax.shard_map(local, mesh=fine, in_specs=in_specs, out_specs=out_specs, check_vma=False)
```

profile of v0, /device:TPU:1, one launch (start us, length us, event | category | flops | bytes accessed | tf_op | source)
XLA Modules:
  0.0 182.9 jit_solution(9903977877614558073)
XLA Ops:
  0.0 1.2 fusion.90
  1.2 1.1 convolution_bitcast_fusion.6
  2.4 1.1 convolution_bitcast_fusion.8
  3.4 27.8 %all-gather = f32[256,64]{1,0:T(8,128)S(1)} all-gather(f32[32,64]{1,0:T(8,128)S(1)} %convolution_bitcast_fusion.8), channel_id=2, replica_groups=mesh['yz'=64,'core'=2,'sub'=4] {'core','sub'}, dimensions={0}, use_global_device_ids=true | all-gather | bytes 73728 | tf_op jit(solution)/shard_map/all_gather | solution.py:86
  31.3 1.3 collective-permute-start.1
  32.6 4.6 %collective-permute-start = (f32[8,32,64]{2,1,0:T(8,128)S(1)}, f32[8,32,64]{2,1,0:T(8,128)}, u32[]{:S(2)}, u32[]{:S(2)}) collective-permute-start(f32[8,32,64]{2,1,0:T(8,128)S(1)} %bitcast.428), channel_id=1, source_target_pairs={{0,8},{8,16},{16,24},{24,32},{32,40},{40,48},{48,56},{56,64},{64,7... | collective-permute-start | bytes 196616 | tf_op jit(solution)/shard_map/ppermute | solution.py:16
  37.9 2.5 %collective-permute-start.3 = (f32[6,32,64]{2,1,0:T(8,128)}, f32[6,32,64]{2,1,0:T(8,128)}, u32[]{:S(2)}, u32[]{:S(2)}) collective-permute-start(f32[6,32,64]{2,1,0:T(8,128)} %pad_maximum_fusion.2), channel_id=1, source_target_pairs={{1,0},{2,1},{3,2},{4,3},{5,4},{6,5},{7,6},{8,7},{9,8},{10,9},{11,1... | collective-permute-start | bytes 147464 | tf_op jit(solution)/shard_map/ppermute | solution.py:17
  40.3 2.8 %collective-permute-start.2 = (f32[6,32,64]{2,1,0:T(8,128)}, f32[6,32,64]{2,1,0:T(8,128)}, u32[]{:S(2)}, u32[]{:S(2)}) collective-permute-start(f32[6,32,64]{2,1,0:T(8,128)} %pad_maximum_fusion.2), channel_id=1, source_target_pairs={{0,1},{1,2},{2,3},{3,4},{4,5},{5,6},{6,7},{7,8},{8,9},{9,10},{10,1... | collective-permute-start | bytes 147464 | tf_op jit(solution)/shard_map/ppermute | solution.py:16
  46.0 1.3 convolution_bitcast_fusion
  49.2 1.9 %collective-permute-start.4 = (f32[2,32,256]{2,1,0:T(8,128)}, f32[2,32,256]{2,1,0:T(8,128)}, u32[]{:S(2)}, u32[]{:S(2)}) collective-permute-start(f32[2,32,256]{2,1,0:T(8,128)} %copy.60), channel_id=1, source_target_pairs={{0,1},{1,2},{2,3},{3,4},{4,5},{5,6},{6,7},{7,8},{8,9},{9,10},{10,1... | collective-permute-start | bytes 196616 | tf_op jit(solution)/shard_map/ppermute | solution.py:16
  51.2 1.1 convolution_bitcast_fusion.3
  52.3 1.1 convolution_bitcast_fusion.5
  53.4 1.1 convolution_bitcast_fusion.7
  54.5 48.6 %all-gather.1 = f32[2048,64]{1,0:T(8,128)} all-gather(f32[32,64]{1,0:T(8,128)S(1)} %convolution_bitcast_fusion.7), channel_id=3, replica_groups=mesh['yz'=64,'core'=2,'sub'=4] {'yz'}, dimensions={0}, use_global_device_ids=true | all-gather | bytes 532480 | tf_op jit(solution)/shard_map/all_gather | solution.py:91
  104.6 2.2 %fusion.112 = f32[32,32,64,1]{2,1,3,0:T(8,128)S(1)} fusion(f32[32,2,32,64]{3,2,1,0:T(8,128)} %bitcast.417, f32[9,2,64,64]{3,2,1,0:T(8,128)} %param.26), kind=kOutput, calls=%fused_computation.163 | convolution fusion | flops 100663296 | bytes 1376256 | tf_op jit(solution)/shard_map/bjkr,jrs->bks/dot_general | solution.py:25
  107.5 1.4 fusion.110
  109.6 1.2 fusion.108
  111.5 1.1 convolution_bitcast_fusion.2
  113.3 1.1 fusion.221
  114.4 1.2 add_add_fusion.1
  118.5 4.6 %select_bitcast_fusion.2 = (f32[1,64,64]{2,1,0:T(8,128)S(1)}, f32[1,64,64]{2,1,0:T(8,128)S(1)}, f32[1,64,64]{2,1,0:T(8,128)}, f32[1,64,64]{2,1,0:T(8,128)}, f32[1,64,64]{2,1,0:T(8,128)}) fusion(f32[10,6,64,64]{3,2,1,0:T(8,128)} %param.28, pred[]{:T(512)} %get-tuple-element.31, pred[]{:T(512)S(6)} %eq.430, pred[]{:T(512)} %get-tuple-element.32, ...), kind=kLoop, calls=%fused_computation.280 | loop fusion | flops 40960 | bytes 229383 | tf_op jit(solution)/shard_map/jit(_where)/select_n | solution.py:41
  123.2 4.6 %select_bitcast_fusion.3 = (f32[1,64,64]{2,1,0:T(8,128)S(1)}, f32[1,64,64]{2,1,0:T(8,128)}, f32[1,64,64]{2,1,0:T(8,128)}, f32[1,64,64]{2,1,0:T(8,128)}, f32[1,64,64]{2,1,0:T(8,128)S(1)}) fusion(f32[10,6,64,64]{3,2,1,0:T(8,128)} %param.28, pred[]{:T(512)S(6)} %eq.430, pred[]{:T(512)} %get-tuple-element.29, pred[]{:T(512)S(6)} %eq.385, ...), kind=kLoop, calls=%fused_computation.281 | loop fusion | flops 40960 | bytes 229384 | tf_op jit(solution)/shard_map/jit(_where)/select_n | solution.py:41
  127.9 3.9 %slice_bitcast_fusion.1 = (f32[64,64]{1,0:T(8,128)S(1)}, f32[1,64,64]{2,1,0:T(8,128)S(1)}, f32[64,64]{1,0:T(8,128)S(1)}, f32[1,64,64]{2,1,0:T(8,128)S(1)}, f32[1...) fusion(f32[10,6,64,64]{3,2,1,0:T(8,128)} %param.28, pred[]{:T(512)S(6)} %eq.394, ...), kind=kLoop, calls=%fused_computation.260 | loop fusion | flops 32768 | bytes 278535 | tf_op jit(solution)/shard_map/squeeze | solution.py:39
  131.8 4.2 %slice_bitcast_fusion.5 = (f32[64,64]{1,0:T(8,128)S(1)}, f32[1,64,64]{2,1,0:T(8,128)S(1)}, f32[64,64]{1,0:T(8,128)S(1)}, f32[1,64,64]{2,1,0:T(8,128)S(1)}, f32[1...) fusion(f32[10,6,64,64]{3,2,1,0:T(8,128)} %param.28, pred[]{:T(512)S(6)} %eq.421, ...), kind=kLoop, calls=%fused_computation.264 | loop fusion | flops 40960 | bytes 278535 | tf_op jit(solution)/shard_map/squeeze | solution.py:39
  136.8 3.5 %slice_bitcast_fusion.3 = (f32[64,64]{1,0:T(8,128)S(1)}, f32[64,64]{1,0:T(8,128)S(1)}, f32[1,64,64]{2,1,0:T(8,128)S(1)}, f32[1,64,64]{2,1,0:T(8,128)S(1)}, f32[6...) fusion(f32[10,6,64,64]{3,2,1,0:T(8,128)} %param.28, ...), kind=kLoop, calls=%fused_computation.262 | loop fusion | flops 32768 | bytes 344070 | tf_op jit(solution)/shard_map/squeeze | solution.py:39
  140.3 1.0 fusion.55
  141.6 4.1 %slice_bitcast_fusion.2 = (f32[64,64]{1,0:T(8,128)S(1)}, f32[1,64,64]{2,1,0:T(8,128)S(1)}, f32[1,64,64]{2,1,0:T(8,128)S(1)}, f32[1,64,64]{2,1,0:T(8,128)S(1)}, f...) fusion(f32[10,6,64,64]{3,2,1,0:T(8,128)} %param.28, pred[]{:T(512)S(6)} %eq.403, ...), kind=kLoop, calls=%fused_computation.261 | loop fusion | flops 40960 | bytes 278535 | tf_op jit(solution)/shard_map/squeeze | solution.py:39
  146.1 4.0 %select_bitcast_fusion.31 = (f32[1,64,64]{2,1,0:T(8,128)}, f32[1,64,64]{2,1,0:T(8,128)}, f32[1,64,64]{2,1,0:T(8,128)}, f32[1,64,64]{2,1,0:T(8,128)}) fusion(f32[10,6,64,64]{3,2,1,0:T(8,128)} %param.28, pred[]{:T(512)S(6)} %eq.367, pred[]{:T(512)} %get-tuple-element.60, pred[]{:T(512)} %get-tuple-element.52, pred[]{:T(512)} %get-tuple-element.55, ...), kind=kLoop, calls=%fused_computation.309 | loop fusion | flops 32768 | bytes 163845 | tf_op jit(solution)/shard_map/jit(_where)/select_n | solution.py:41
  153.3 16.3 %collective-permute-start.5 = (f32[2,32,256]{2,1,0:T(8,128)}, f32[2,32,256]{2,1,0:T(8,128)S(1)}, u32[]{:S(2)}, u32[]{:S(2)}) collective-permute-start(f32[2,32,256]{2,1,0:T(8,128)} %copy.61), channel_id=1, source_target_pairs={{1,0},{2,1},{3,2},{4,3},{5,4},{6,5},{7,6},{8,7},{9,8},{10,9},{11,1... | collective-permute-start | bytes 196616 | tf_op jit(solution)/shard_map/ppermute | solution.py:17
  173.1 1.1 pad_maximum_fusion
  174.2 1.4 fusion.117
  175.8 1.2 convolution_bitcast_fusion.1
  (174 shorter events, 25.8 us)
Async XLA Ops:
  0.0 45.4 %copy-start = (bf16[4,5,256,256]{3,2,1,0:T(8,128)(2,1)S(1)}, bf16[4,5,256,256]{3,2,1,0:T(8,128)(2,1)}, u32[]{:S(2)}) copy-start(bf16[4,5,256,256]{3,2,1,0:T(8,128)(2,1)} %param.21) | copy-start | bytes 7864324
  1.2 36.0 %copy-start.3 = (f32[4,32,64]{2,1,0:T(8,128)}, f32[4,32,64]{2,1,0:T(8,128)S(1)}, u32[]{:S(2)}) copy-start(f32[4,32,64]{2,1,0:T(8,128)S(1)} %fusion.90) | copy-start | bytes 98308
  2.4 35.5 %copy-start.5 = (f32[2,32,64]{2,1,0:T(8,128)}, f32[2,32,64]{2,1,0:T(8,128)S(1)}, u32[]{:S(2)}) copy-start(f32[2,32,64]{2,1,0:T(8,128)S(1)} %convolution_bitcast_fusion.6) | copy-start | bytes 49156
  31.3 141.8 %collective-permute-start.1 = (f32[8,32,64]{2,1,0:T(8,128)S(1)}, f32[8,32,64]{2,1,0:T(8,128)}, u32[]{:S(2)}, u32[]{:S(2)}) collective-permute-start(f32[8,32,64]{2,1,0:T(8,128)S(1)} %bitcast.427), channel_id=1, source_target_pairs={{8,0},{16,8},{24,16},{32,24},{40,32},{48,40},{56,48},{64,56},{72,6... | collective-permute-start | bytes 196616 | tf_op jit(solution)/shard_map/ppermute | solution.py:17
  32.6 140.5 %collective-permute-start = (f32[8,32,64]{2,1,0:T(8,128)S(1)}, f32[8,32,64]{2,1,0:T(8,128)}, u32[]{:S(2)}, u32[]{:S(2)}) collective-permute-start(f32[8,32,64]{2,1,0:T(8,128)S(1)} %bitcast.428), channel_id=1, source_target_pairs={{0,8},{8,16},{16,24},{24,32},{32,40},{40,48},{48,56},{56,64},{64,7... | collective-permute-start | bytes 196616 | tf_op jit(solution)/shard_map/ppermute | solution.py:16
  37.9 115.4 %collective-permute-start.3 = (f32[6,32,64]{2,1,0:T(8,128)}, f32[6,32,64]{2,1,0:T(8,128)}, u32[]{:S(2)}, u32[]{:S(2)}) collective-permute-start(f32[6,32,64]{2,1,0:T(8,128)} %pad_maximum_fusion.2), channel_id=1, source_target_pairs={{1,0},{2,1},{3,2},{4,3},{5,4},{6,5},{7,6},{8,7},{9,8},{10,9},{11,1... | collective-permute-start | bytes 147464 | tf_op jit(solution)/shard_map/ppermute | solution.py:17
  40.3 130.0 %collective-permute-start.2 = (f32[6,32,64]{2,1,0:T(8,128)}, f32[6,32,64]{2,1,0:T(8,128)}, u32[]{:S(2)}, u32[]{:S(2)}) collective-permute-start(f32[6,32,64]{2,1,0:T(8,128)} %pad_maximum_fusion.2), channel_id=1, source_target_pairs={{0,1},{1,2},{2,3},{3,4},{4,5},{5,6},{6,7},{7,8},{8,9},{9,10},{10,1... | collective-permute-start | bytes 147464 | tf_op jit(solution)/shard_map/ppermute | solution.py:16
  49.2 131.5 %collective-permute-start.4 = (f32[2,32,256]{2,1,0:T(8,128)}, f32[2,32,256]{2,1,0:T(8,128)}, u32[]{:S(2)}, u32[]{:S(2)}) collective-permute-start(f32[2,32,256]{2,1,0:T(8,128)} %copy.60), channel_id=1, source_target_pairs={{0,1},{1,2},{2,3},{3,4},{4,5},{5,6},{6,7},{7,8},{8,9},{9,10},{10,1... | collective-permute-start | bytes 196616 | tf_op jit(solution)/shard_map/ppermute | solution.py:16
  115.6 20.5 %copy-start.38 = (f32[1,32,64]{2,1,0:T(8,128)S(1)}, f32[1,32,64]{2,1,0:T(8,128)}, u32[]{:S(2)}) copy-start(f32[1,32,64]{2,1,0:T(8,128)} %get-tuple-element.136) | copy-start | bytes 24580
  115.6 20.5 %copy-start.39 = (f32[1,32,64]{2,1,0:T(8,128)S(1)}, f32[1,32,64]{2,1,0:T(8,128)}, u32[]{:S(2)}) copy-start(f32[1,32,64]{2,1,0:T(8,128)} %get-tuple-element.137) | copy-start | bytes 24580
  115.6 20.5 %copy-start.40 = (f32[1,32,64]{2,1,0:T(8,128)S(1)}, f32[1,32,64]{2,1,0:T(8,128)}, u32[]{:S(2)}) copy-start(f32[1,32,64]{2,1,0:T(8,128)} %get-tuple-element.138) | copy-start | bytes 24580
  115.6 20.7 %copy-start.41 = (f32[1,32,64]{2,1,0:T(8,128)S(1)}, f32[1,32,64]{2,1,0:T(8,128)}, u32[]{:S(2)}) copy-start(f32[1,32,64]{2,1,0:T(8,128)} %get-tuple-element.131) | copy-start | bytes 24580
  115.6 20.7 %copy-start.42 = (f32[1,32,64]{2,1,0:T(8,128)S(1)}, f32[1,32,64]{2,1,0:T(8,128)}, u32[]{:S(2)}) copy-start(f32[1,32,64]{2,1,0:T(8,128)} %get-tuple-element.132) | copy-start | bytes 24580
  115.6 20.7 %copy-start.43 = (f32[1,32,64]{2,1,0:T(8,128)S(1)}, f32[1,32,64]{2,1,0:T(8,128)}, u32[]{:S(2)}) copy-start(f32[1,32,64]{2,1,0:T(8,128)} %get-tuple-element.133) | copy-start | bytes 24580
  115.7 20.7 %copy-start.44 = (f32[1,32,64]{2,1,0:T(8,128)S(1)}, f32[1,32,64]{2,1,0:T(8,128)}, u32[]{:S(2)}) copy-start(f32[1,32,64]{2,1,0:T(8,128)} %get-tuple-element.134) | copy-start | bytes 24580
  123.1 22.5 %copy-start.33 = (f32[1,32,64]{2,1,0:T(8,128)S(1)}, f32[1,32,64]{2,1,0:T(8,128)}, u32[]{:S(2)}) copy-start(f32[1,32,64]{2,1,0:T(8,128)} %get-tuple-element.143) | copy-start | bytes 24580
  123.1 22.5 %copy-start.34 = (f32[1,32,64]{2,1,0:T(8,128)S(1)}, f32[1,32,64]{2,1,0:T(8,128)}, u32[]{:S(2)}) copy-start(f32[1,32,64]{2,1,0:T(8,128)} %get-tuple-element.144) | copy-start | bytes 24580
  123.1 22.5 %copy-start.35 = (f32[1,32,64]{2,1,0:T(8,128)S(1)}, f32[1,32,64]{2,1,0:T(8,128)}, u32[]{:S(2)}) copy-start(f32[1,32,64]{2,1,0:T(8,128)} %get-tuple-element.145) | copy-start | bytes 24580
  123.2 22.5 %copy-start.36 = (f32[1,32,64]{2,1,0:T(8,128)S(1)}, f32[1,32,64]{2,1,0:T(8,128)}, u32[]{:S(2)}) copy-start(f32[1,32,64]{2,1,0:T(8,128)} %get-tuple-element.146) | copy-start | bytes 24580
  127.8 22.3 %copy-start.50 = (s32[2,4]{1,0:T(2,128)S(1)}, s32[2,4]{1,0:T(2,128)}, u32[]{:S(2)}) copy-start(s32[2,4]{1,0:T(2,128)} %param.24) | copy-start | bytes 100
  127.8 22.5 %copy-start.45 = (s32[4,4]{1,0:T(4,128)S(1)}, s32[4,4]{1,0:T(4,128)}, u32[]{:S(2)}) copy-start(s32[4,4]{1,0:T(4,128)} %param.23) | copy-start | bytes 196
  127.8 22.5 %copy-start.46 = (s32[4]{0:T(128)S(1)}, s32[4]{0:T(128)}, u32[]{:S(2)}) copy-start(s32[4]{0:T(128)} %get-tuple-element.175) | copy-start | bytes 52
  127.8 22.5 %copy-start.47 = (s32[4]{0:T(128)S(1)}, s32[4]{0:T(128)}, u32[]{:S(2)}) copy-start(s32[4]{0:T(128)} %get-tuple-element.176) | copy-start | bytes 52
  127.8 22.5 %copy-start.48 = (s32[4]{0:T(128)S(1)}, s32[4]{0:T(128)}, u32[]{:S(2)}) copy-start(s32[4]{0:T(128)} %get-tuple-element.177) | copy-start | bytes 52
  127.8 22.5 %copy-start.49 = (s32[4]{0:T(128)S(1)}, s32[4]{0:T(128)}, u32[]{:S(2)}) copy-start(s32[4]{0:T(128)} %get-tuple-element.178) | copy-start | bytes 52
  127.8 22.7 %copy-start.29 = (f32[1,32,64]{2,1,0:T(8,128)S(1)}, f32[1,32,64]{2,1,0:T(8,128)}, u32[]{:S(2)}) copy-start(f32[1,32,64]{2,1,0:T(8,128)} %get-tuple-element.147) | copy-start | bytes 24580
  127.9 22.7 %copy-start.30 = (f32[1,32,64]{2,1,0:T(8,128)S(1)}, f32[1,32,64]{2,1,0:T(8,128)}, u32[]{:S(2)}) copy-start(f32[1,32,64]{2,1,0:T(8,128)} %get-tuple-element.148) | copy-start | bytes 24580
  127.9 22.7 %copy-start.31 = (f32[1,32,64]{2,1,0:T(8,128)S(1)}, f32[1,32,64]{2,1,0:T(8,128)}, u32[]{:S(2)}) copy-start(f32[1,32,64]{2,1,0:T(8,128)} %get-tuple-element.149) | copy-start | bytes 24580
  127.9 22.7 %copy-start.32 = (f32[1,32,64]{2,1,0:T(8,128)S(1)}, f32[1,32,64]{2,1,0:T(8,128)}, u32[]{:S(2)}) copy-start(f32[1,32,64]{2,1,0:T(8,128)} %get-tuple-element.150) | copy-start | bytes 24580
  141.4 29.7 %copy-start.6 = (f32[2,32,64]{2,1,0:T(8,128)S(1)}, f32[2,32,64]{2,1,0:T(8,128)}, u32[]{:S(2)}) copy-start(f32[2,32,64]{2,1,0:T(8,128)} %copy-done.5) | copy-start | bytes 49156
  141.6 31.3 %copy-start.4 = (f32[4,32,64]{2,1,0:T(8,128)S(1)}, f32[4,32,64]{2,1,0:T(8,128)}, u32[]{:S(2)}) copy-start(f32[4,32,64]{2,1,0:T(8,128)} %copy-done.3) | copy-start | bytes 98308
  153.3 28.7 %collective-permute-start.5 = (f32[2,32,256]{2,1,0:T(8,128)}, f32[2,32,256]{2,1,0:T(8,128)S(1)}, u32[]{:S(2)}, u32[]{:S(2)}) collective-permute-start(f32[2,32,256]{2,1,0:T(8,128)} %copy.61), channel_id=1, source_target_pairs={{1,0},{2,1},{3,2},{4,3},{5,4},{6,5},{7,6},{8,7},{9,8},{10,9},{11,1... | collective-permute-start | bytes 196616 | tf_op jit(solution)/shard_map/ppermute | solution.py:17
  (27 other events, 209.7 us)
where the time goes:
time: 185 us; the launch traced here: 183 us
  blocking collectives  76.5 us (41%)
  other arithmetic  39.1 us (21%)
  starting transfers between devices  29.4 us (16%)
  matrix products  23.8 us (13%)
  local copies, waits for them, and re-layouts  12.9 us (7%)
    all_gather x1, blocking collectives, local(): top = [lax.all_gather(own5[0], 'yz', axis=0, tiled=False)]  48.6 us
    all_gather x1, blocking collectives, local(): grp = lax.all_gather(a2[0], GROUP, axis=0, tiled=False)  27.8 us
    ppermute x3, starting transfers between devices, padded(): after = lax.ppermute(shard[:width], axis, down)  20 us
    select_n x5, other arithmetic, window_coupling(): mats.append(jnp.where(hits[i][:, None, None], chosen, 0.0))  14.9 us
    dot_general x11, matrix products, halve(): return jnp.einsum('bjkr,jrs->bks', paired, transfer, precision=highest)  14.1 us
    ppermute x3, starting transfers between devices, padded(): before = lax.ppermute(shard[length - width:], axis, up)  9.37 us
    squeeze x2, other arithmetic, window_coupling(): level_coupling[odd_cls[i]]  8.34 us
    squeeze x2, other arithmetic, window_coupling(): level_coupling[even_cls[i]]  7.43 us
  transfers between devices with their start and end apart: 6, of which 0 were waited for; matrix products, arithmetic and copies ran while one was open for 39% of the time, Pallas kernels for 0%

commit v1 on v0

--- a/solution.py
+++ b/solution.py
@@ -25,30 +25,23 @@
     return jnp.einsum("bjkr,jrs->bks", paired, transfer, precision=highest)
 
 
-def window_coupling(windows, bases, rows, odd, level_coupling):
-    picks = (0, 1, 4, 5)
-    stacked = jnp.concatenate([windows[:, w] for w in picks], axis=-1)
-    hits = [
-        jnp.any((rows == (bases + w)[:, None]) & (rows >= 0), axis=1) for w in picks
-    ]
-    even_cls = (1, 2, 4, 5)
-    odd_cls = (0, 1, 3, 4)
-    mats = []
-    for i in range(4):
-        chosen = jnp.where(
-            odd[:, None, None], level_coupling[odd_cls[i]], level_coupling[even_cls[i]]
-        )
-        mats.append(jnp.where(hits[i][:, None, None], chosen, 0.0))
-    matrix = jnp.concatenate(mats, axis=1)
-    return jnp.einsum("bkr,brs->bks", stacked, matrix, precision=highest)
-
-
-def one_box(level_array, offset, box, row, level_coupling):
+def class_blocks(windows, bases, rows, odd):
+    masked = []
+    for w in (0, 1, 4, 5):
+        hit = jnp.any((rows == (bases + w)[:, None]) & (rows >= 0), axis=1)
+        masked.append(jnp.where(hit[:, None, None], windows[:, w], 0.0))
+    zero = jnp.zeros_like(masked[0])
+    m0, m1, m4, m5 = masked
+    odd_blocks = jnp.concatenate([m0, m1, zero, m4, m5, zero], axis=-1)
+    even_blocks = jnp.concatenate([zero, m0, m1, zero, m4, m5], axis=-1)
+    return jnp.where(odd[:, None, None], odd_blocks, even_blocks)
+
+
+def one_box(level_array, offset, box, row):
     base = 2 * (box >> 1) - 2
     win = lax.dynamic_slice_in_dim(level_array, base - offset, 6, axis=0)
-    return window_coupling(
-        win[None], jnp.reshape(base, (1,)), row[None], jnp.reshape(box & 1, (1,)) == 1,
-        level_coupling,
+    return class_blocks(
+        win[None], jnp.reshape(base, (1,)), row[None], jnp.reshape(box & 1, (1,)) == 1
     )[0]
 
 
@@ -83,12 +76,19 @@
     a1 = halve(a0, row_transfer[0])
     a2 = halve(a1, row_transfer[1])
 
-    grp = lax.all_gather(a2[0], GROUP, axis=0, tiled=False)
-    up_levels = [grp]
+    slot = jnp.arange(group_size, dtype=jnp.int32) == in_group
+    grp = lax.psum(jnp.where(slot[:, None, None], a2, 0.0), GROUP)
+    share = a2[0]
     for height in range(2, 5):
-        up_levels.append(halve(up_levels[-1], row_transfer[height]))
-    own5 = up_levels[-1]
-    top = [lax.all_gather(own5[0], "yz", axis=0, tiled=False)]
+        bit = (device >> (height - 2)) & 1
+        matrix = row_transfer[height].reshape(2 * basis_rank, basis_rank)
+        share = jnp.dot(
+            jnp.concatenate([jnp.where(bit == 0, share, 0.0), jnp.where(bit == 1, share, 0.0)], axis=-1),
+            matrix,
+            precision=highest,
+        )
+    gslot = jnp.arange(groups, dtype=jnp.int32) == group
+    top = [lax.psum(jnp.where(gslot[:, None, None], share[None], 0.0), ALL)]
     for height in range(5, levels_total - 1):
         top.append(halve(top[-1], row_transfer[height]))
 
@@ -129,35 +129,46 @@
     def top_row(height, box):
         return lax.dynamic_index_in_dim(far_top, starts[height] + box, 0, keepdims=False)
 
-    g = {}
+    blocks_top = []
     for height in range(5, levels_total):
-        arr = top[height - 5]
-        arr = jnp.pad(arr, ((2, 2), (0, 0), (0, 0)))
+        arr = jnp.pad(top[height - 5], ((2, 2), (0, 0), (0, 0)))
         box = group >> (height - 5)
-        g[height] = one_box(arr, -2, box, top_row(height, box), coupling[height])
+        blocks_top.append(one_box(arr, -2, box, top_row(height, box)))
+    cpl = coupling.reshape(levels_total, 6 * basis_rank, basis_rank)
+    g_top = jnp.einsum("lkc,lcs->lks", jnp.stack(blocks_top), cpl[5:], precision=highest)
+    blocks_mid = []
     for height in range(2, 5):
-        arr = ext[height - 2]
         box = device >> (height - 2)
         offset = (group - 1) * (group_size >> (height - 2))
-        g[height] = one_box(arr, offset, box, top_row(height, box), coupling[height])
+        blocks_mid.append(one_box(ext[height - 2], offset, box, top_row(height, box)))
+    g_mid = jnp.einsum("lkc,lcs->lks", jnp.stack(blocks_mid), cpl[2:5], precision=highest)
+    g = {height: g_top[height - 5] for height in range(5, levels_total)}
+    g.update({height: g_mid[height - 2] for height in range(2, 5)})
 
     expansion = g[levels_total - 1]
     for height in range(levels_total - 2, 1, -1):
-        box = device >> (height - 2)
-        matrix = lax.dynamic_index_in_dim(col_transfer[height], box & 1, 0, keepdims=False)
-        expansion = g[height] + jnp.dot(expansion, matrix, precision=highest)
+        bit = (device >> (height - 2)) & 1
+        matrix = col_transfer[height].reshape(2 * basis_rank, basis_rank)
+        spread_b = jnp.concatenate(
+            [jnp.where(bit == 0, expansion, 0.0), jnp.where(bit == 1, expansion, 0.0)], axis=-1
+        )
+        expansion = g[height] + jnp.dot(spread_b, matrix, precision=highest)
 
     odd1 = jnp.array([False, True])
     bases1 = jnp.full((2,), 2 * device - 2, jnp.int32)
     win1 = jnp.stack([ext1[0:6], ext1[0:6]], axis=0)
-    g1 = window_coupling(win1, bases1, far_pair, odd1, coupling[1])
+    g1 = jnp.einsum(
+        "bkc,cs->bks", class_blocks(win1, bases1, far_pair, odd1), cpl[1], precision=highest
+    )
     b1 = jnp.einsum("kr,jrs->jks", expansion, col_transfer[1], precision=highest) + g1
 
     odd0 = jnp.array([False, True, False, True])
     local_starts = (2, 2, 4, 4)
     bases0 = first_leaf + jnp.array([0, 0, 2, 2], jnp.int32) - 2
-    win0 = jnp.stack([ext0[s : s + 6] for s in local_starts], axis=0)
-    g0 = window_coupling(win0, bases0, far_leaf, odd0, coupling[0])
+    win0 = jnp.stack([ext0[st : st + 6] for st in local_starts], axis=0)
+    g0 = jnp.einsum(
+        "bkc,cs->bks", class_blocks(win0, bases0, far_leaf, odd0), cpl[0], precision=highest
+    )
     pushed = jnp.einsum("jkr,crs->jcks", b1, col_transfer[0], precision=highest)
     b0 = pushed.reshape(leaves, probe_count, basis_rank) + g0
 

time: 185 us -> 433 us (2.34)
  waiting for transfers between devices: 0.02 us -> 291 us
  blocking collectives: 76.5 us -> 0 us
  local copies, waits for them, and re-layouts: 12.9 us -> 35.9 us
  between operations: 1.25 us -> 14.1 us
  starting transfers between devices: 29.4 us -> 18.8 us
  matrix products: 23.8 us -> 32.7 us
    psum x0 -> x2, waiting for transfers between devices: none -> 291 us  [the longest x1 246 us: local(): top = [lax.psum(jnp.where(gslot[:, None, None], share[None], 0.0), ALL)]]
    all_gather x2 -> x0, blocking collectives: 76.5 us -> none  [the longest x1 48.6 us: local(): top = [lax.all_gather(own5[0], 'yz', axis=0, tiled=False)]]
    concatenate x1 -> x5, other arithmetic: 1.06 us -> 21.9 us  [class_blocks(): odd_blocks = jnp.concatenate([m0, m1, zero, m4, m5, zero], axis=-1)]
    concatenate x0 -> x21, local copies, waits for them, and re-layouts: none -> 20 us  [the longest x10 10 us: class_blocks(): even_blocks = jnp.concatenate([zero, m0, m1, zero, m4, m5], axis=-1)]
    squeeze x6 -> x0, other arithmetic: 15.8 us -> none  [the longest x2 8.34 us: window_coupling(): level_coupling[odd_cls[i]]]
    select_n x5 -> x9, other arithmetic: 14.9 us -> 3 us  [the longest x1 1.18 us: local(): top = [lax.psum(jnp.where(gslot[:, None, None], share[None], 0.0), ALL)]]
    dot_general x17 -> x14, matrix products: 4.5 us -> 16.2 us  [the longest x7 7.38 us: local(): expansion = g[height] + jnp.dot(spread_b, matrix, precision=highest)]
    ppermute x3, starting transfers between devices: 20 us -> 9.87 us  [padded(): after = lax.ppermute(shard[:width], axis, down)]
  transfers between devices with their start and end apart: 6 -> 8, of which waited for: 0 -> 2; matrix products, arithmetic and copies ran while one was open for 39% -> 13% of each run, Pallas kernels for 0% -> 0%
where the time goes in v1:
time: 433 us; the launch traced here: 430 us
  waiting for transfers between devices  291 us (67%)
  other arithmetic  37.7 us (9%)
  local copies, waits for them, and re-layouts  35.9 us (8%)
  matrix products  32.7 us (8%)
  starting transfers between devices  18.8 us (4%)
  between operations  14.1 us (3%)
    psum x1, waiting for transfers between devices, local(): top = [lax.psum(jnp.where(gslot[:, None, None], share[None], 0.0), ALL)]  246 us
    psum x1, waiting for transfers between devices, local(): grp = lax.psum(jnp.where(slot[:, None, None], a2, 0.0), GROUP)  44.1 us
    concatenate x5, other arithmetic, class_blocks(): odd_blocks = jnp.concatenate([m0, m1, zero, m4, m5, zero], axis=-1)  21.9 us
    dot_general x8, matrix products, halve(): return jnp.einsum('bjkr,jrs->bks', paired, transfer, precision=highest)  11.4 us
    concatenate x10, local copies, waits for them, and re-layouts, class_blocks(): even_blocks = jnp.concatenate([zero, m0, m1, zero, m4, m5], axis=-1)  10 us
    ppermute x3, starting transfers between devices, padded(): after = lax.ppermute(shard[:width], axis, down)  9.87 us
    concatenate x10, local copies, waits for them, and re-layouts, class_blocks(): odd_blocks = jnp.concatenate([m0, m1, zero, m4, m5, zero], axis=-1)  9.08 us
    ppermute x3, starting transfers between devices, padded(): before = lax.ppermute(shard[length - width:], axis, up)  8.91 us
  transfers between devices with their start and end apart: 8, of which 2 were waited for; matrix products, arithmetic and copies ran while one was open for 13% of the time, Pallas kernels for 0%

profile of v1, /device:TPU:1, one launch (start us, length us, event | category | flops | bytes accessed | tf_op | source)
XLA Modules:
  0.0 429.8 jit_solution(217140111133729186)
XLA Ops:
  9.5 3.9 collective-permute-start.2
  13.5 3.8 collective-permute-start.3
  17.2 1.7 broadcast_select_fusion.22
  25.6 1.9 collective-permute-start.4
  28.1 4.8 %collective-permute-start.5 = (f32[2,32,256]{2,1,0:T(8,128)}, f32[2,32,256]{2,1,0:T(8,128)}, u32[]{:S(2)}, u32[]{:S(2)}) collective-permute-start(f32[2,32,256]{2,1,0:T(8,128)} %copy.64), channel_id=1, source_target_pairs={{1,0},{2,1},{3,2},{4,3},{5,4},{6,5},{7,6},{8,7},{9,8},{10,9},{11,1... | collective-permute-start | bytes 196616 | tf_op jit(solution)/shard_map/ppermute | solution.py:17
  33.0 1.6 fusion.148
  39.8 1.8 fusion.146
  44.0 2.3 slice.346
  49.2 44.1 %all-reduce.8.cloned.1.call-done = f32[8,32,64]{2,1,0:T(8,128)} async-done(((f32[8,32,64]{2,1,0:T(8,128)}), f32[8,32,64]{2,1,0:T(8,128)}) %all-reduce.8.cloned.1.call-update) | async-done | bytes 65552 | tf_op jit(solution)/shard_map/psum | solution.py:80
  93.3 3.1 collective-permute-start
  96.4 1.3 collective-permute-start.1
  103.5 1.7 concatenate.368
  109.8 1.3 fusion.43
  111.2 5.6 %fusion.87 = (f32[1,32,64]{2,1,0:T(8,128)S(1)}, f32[1,32,64]{2,1,0:T(8,128)S(1)}, f32[1,32,64]{2,1,0:T(8,128)}, f32[1,32,64]{2,1,0:T(8,128)}, f32[1,32,64]{2,1,0...) fusion(f32[1,6,32,64]{3,2,1,0:T(8,128)S(1)} %dynamic-slice_bitcast_fusion, ...), kind=kLoop, calls=%fused_computation.171 | loop fusion | flops 16384 | bytes 131080 | tf_op jit(solution)/shard_map/concatenate | solution.py:35
  119.0 1.4 concatenate.314
  120.5 1.4 concatenate.313
  123.1 2.5 fusion.83
  127.8 246.5 %all-reduce.10.cloned.1.call-done = f32[64,32,64]{2,1,0:T(8,128)} async-done(((f32[64,32,64]{2,1,0:T(8,128)}), f32[64,32,64]{2,1,0:T(8,128)}) %all-reduce.10.cloned.1.call-update) | async-done | bytes 524304 | tf_op jit(solution)/shard_map/psum | solution.py:91
  374.2 2.3 fusion.40
  376.5 1.4 fusion.38
  380.4 5.6 %fusion.63 = (f32[1,32,64]{2,1,0:T(8,128)}, f32[1,32,64]{2,1,0:T(8,128)}, f32[1,32,64]{2,1,0:T(8,128)}, f32[1,32,64]{2,1,0:T(8,128)}, f32[1,32,64]{2,1,0:T(8,128...) fusion(f32[1,6,32,64]{3,2,1,0:T(8,128)S(1)} %fusion.14, pred[]{:T(512)} %get-tuple-element.29, ...), kind=kLoop, calls=%fused_computation.120 | loop fusion | flops 16384 | bytes 131080 | tf_op jit(solution)/shard_map/concatenate | solution.py:35
  386.0 1.5 concatenate.353
  387.5 1.5 concatenate.352
  389.0 5.7 %fusion.67 = (f32[1,32,64]{2,1,0:T(8,128)S(1)}, f32[1,32,64]{2,1,0:T(8,128)S(1)}, f32[1,32,64]{2,1,0:T(8,128)S(1)}, f32[1,32,64]{2,1,0:T(8,128)S(1)}, f32[1,32,6...) fusion(f32[1,6,32,64]{3,2,1,0:T(8,128)S(1)} %fusion.15, ...), kind=kLoop, calls=%fused_computation.128 | loop fusion | flops 16384 | bytes 131080 | tf_op jit(solution)/shard_map/concatenate | solution.py:35
  396.1 2.6 fusion.71
  398.9 1.5 concatenate.335
  400.4 1.5 concatenate.334
  401.8 1.5 concatenate.329
  403.3 1.5 concatenate.328
  408.1 1.9 fusion.150
  418.5 1.2 fusion.2
  420.8 1.3 fusion.1
  (136 shorter events, 54.1 us)
Async XLA Ops:
  6.5 15.9 %copy-start = (bf16[4,5,256,256]{3,2,1,0:T(8,128)(2,1)S(1)}, bf16[4,5,256,256]{3,2,1,0:T(8,128)(2,1)}, u32[]{:S(2)}) copy-start(bf16[4,5,256,256]{3,2,1,0:T(8,128)(2,1)} %param.21) | copy-start | bytes 7864324
  6.5 86.8 %all-reduce.8.cloned.1.call-start = ((), (), s32[]{:S(2)}) async-start(), calls=%async_computation | async-start | bytes 262144 | tf_op jit(solution)/shard_map/psum | solution.py:80
  8.9 13.6 %copy-start.10 = (f32[2,32,64]{2,1,0:T(8,128)}, f32[2,32,64]{2,1,0:T(8,128)S(1)}, u32[]{:S(2)}) copy-start(f32[2,32,64]{2,1,0:T(8,128)S(1)} %convolution_bitcast_fusion.4) | copy-start | bytes 49156
  9.5 86.9 %collective-permute-start.2 = (f32[6,32,64]{2,1,0:T(8,128)}, f32[6,32,64]{2,1,0:T(8,128)}, u32[]{:S(2)}, u32[]{:S(2)}) collective-permute-start(f32[6,32,64]{2,1,0:T(8,128)} %pad_maximum_fusion.1), channel_id=1, source_target_pairs={{0,1},{1,2},{2,3},{3,4},{4,5},{5,6},{6,7},{7,8},{8,9},{9,10},{10,1... | collective-permute-start | bytes 147464 | tf_op jit(solution)/shard_map/ppermute | solution.py:16
  13.5 85.0 %collective-permute-start.3 = (f32[6,32,64]{2,1,0:T(8,128)}, f32[6,32,64]{2,1,0:T(8,128)}, u32[]{:S(2)}, u32[]{:S(2)}) collective-permute-start(f32[6,32,64]{2,1,0:T(8,128)} %pad_maximum_fusion.1), channel_id=1, source_target_pairs={{1,0},{2,1},{3,2},{4,3},{5,4},{6,5},{7,6},{8,7},{9,8},{10,9},{11,1... | collective-permute-start | bytes 147464 | tf_op jit(solution)/shard_map/ppermute | solution.py:17
  19.7 354.6 %all-reduce.10.cloned.1.call-start = ((), (), s32[]{:S(2)}) async-start(), calls=%async_computation.1 | async-start | bytes 2097152 | tf_op jit(solution)/shard_map/psum | solution.py:91
  21.8 1.2 copy-start.18
  23.0 16.0 %copy-start.7 = (f32[9,2,64,64]{3,2,1,0:T(8,128)S(1)}, f32[9,2,64,64]{3,2,1,0:T(8,128)}, u32[]{:S(2)}) copy-start(f32[9,2,64,64]{3,2,1,0:T(8,128)} %param.27) | copy-start | bytes 884740
  25.6 79.6 %collective-permute-start.4 = (f32[2,32,256]{2,1,0:T(8,128)}, f32[2,32,256]{2,1,0:T(8,128)}, u32[]{:S(2)}, u32[]{:S(2)}) collective-permute-start(f32[2,32,256]{2,1,0:T(8,128)} %copy.63), channel_id=1, source_target_pairs={{0,1},{1,2},{2,3},{3,4},{4,5},{5,6},{6,7},{7,8},{8,9},{9,10},{10,1... | collective-permute-start | bytes 196616 | tf_op jit(solution)/shard_map/ppermute | solution.py:16
  28.1 78.0 %collective-permute-start.5 = (f32[2,32,256]{2,1,0:T(8,128)}, f32[2,32,256]{2,1,0:T(8,128)}, u32[]{:S(2)}, u32[]{:S(2)}) collective-permute-start(f32[2,32,256]{2,1,0:T(8,128)} %copy.64), channel_id=1, source_target_pairs={{1,0},{2,1},{3,2},{4,3},{5,4},{6,5},{7,6},{8,7},{9,8},{10,9},{11,1... | collective-permute-start | bytes 196616 | tf_op jit(solution)/shard_map/ppermute | solution.py:17
  39.0 7.4 %copy-start.17 = (s32[1020,4]{0,1:T(4,128)S(1)}, s32[1020,4]{0,1:T(4,128)}, u32[]{:S(2)}) copy-start(s32[1020,4]{0,1:T(4,128)} %param.25) | copy-start | bytes 48964
  39.8 59.4 %copy-start.11 = (f32[2,32,64]{2,1,0:T(8,128)S(1)}, f32[2,32,64]{2,1,0:T(8,128)}, u32[]{:S(2)}) copy-start(f32[2,32,64]{2,1,0:T(8,128)} %copy-done.10) | copy-start | bytes 49156
  93.3 13.7 %collective-permute-start = (f32[8,32,64]{2,1,0:T(8,128)}, f32[8,32,64]{2,1,0:T(8,128)}, u32[]{:S(2)}, u32[]{:S(2)}) collective-permute-start(f32[8,32,64]{2,1,0:T(8,128)} %all-reduce.8.cloned.1.call-done), channel_id=1, source_target_pairs={{0,8},{8,16},{16,24},{24,32},{32,40},{40,48},{48,56},{56,64},{64,7... | collective-permute-start | bytes 196616 | tf_op jit(solution)/shard_map/ppermute | solution.py:16
  96.4 12.5 %collective-permute-start.1 = (f32[8,32,64]{2,1,0:T(8,128)}, f32[8,32,64]{2,1,0:T(8,128)}, u32[]{:S(2)}, u32[]{:S(2)}) collective-permute-start(f32[8,32,64]{2,1,0:T(8,128)} %all-reduce.8.cloned.1.call-done), channel_id=1, source_target_pairs={{8,0},{16,8},{24,16},{32,24},{40,32},{48,40},{56,48},{64,56},{72,6... | collective-permute-start | bytes 196616 | tf_op jit(solution)/shard_map/ppermute | solution.py:17
  101.1 1.5 copy-start.8
  101.2 1.5 copy-start.9
  103.5 23.2 %slice-start = ((f32[10,6,64,64]{3,2,1,0:T(8,128)}), f32[3,6,64,64]{3,2,1,0:T(8,128)S(1)}, s32[]{:S(2)}) async-start(f32[10,6,64,64]{3,2,1,0:T(8,128)} %param.28), calls=%async_computation.2 | async-start | bytes 1179648 | tf_op jit(solution)/shard_map/slice | solution.py:144
  107.0 2.9 copy-start.2
  116.8 0.6 copy-start.13
  116.8 0.6 copy-start.14
  116.8 0.6 copy-start.15
  374.2 6.2 %copy-start.1 = (f32[64,32,64]{2,1,0:T(8,128)S(1)}, f32[64,32,64]{2,1,0:T(8,128)}, u32[]{:S(2)}) copy-start(f32[64,32,64]{2,1,0:T(8,128)} %all-reduce.10.cloned.1.call-done) | copy-start | bytes 1572868
  389.0 26.5 %copy-start.12 = (f32[1,2,64,64]{3,2,1,0:T(8,128)S(1)}, f32[1,2,64,64]{3,2,1,0:T(8,128)}, u32[]{:S(2)}) copy-start(f32[1,2,64,64]{3,2,1,0:T(8,128)} %get-tuple-element.73) | copy-start | bytes 98308
  389.0 29.5 %copy-start.4 = (f32[1,6,64,64]{3,2,1,0:T(8,128)S(1)}, f32[1,6,64,64]{3,2,1,0:T(8,128)}, u32[]{:S(2)}) copy-start(f32[1,6,64,64]{3,2,1,0:T(8,128)} %get-tuple-element.70) | copy-start | bytes 294916
  396.1 24.7 %copy-start.5 = (f32[1,6,64,64]{3,2,1,0:T(8,128)S(1)}, f32[1,6,64,64]{3,2,1,0:T(8,128)}, u32[]{:S(2)}) copy-start(f32[1,6,64,64]{3,2,1,0:T(8,128)} %get-tuple-element.69) | copy-start | bytes 294916
  396.1 24.7 %copy-start.6 = (f32[4,32,384]{2,1,0:T(8,128)S(1)}, f32[4,32,384]{2,1,0:T(8,128)}, u32[]{:S(2)}) copy-start(f32[4,32,384]{2,1,0:T(8,128)} %concatenate.367) | copy-start | bytes 589828
  398.9 23.3 %copy-start.3 = (f32[4,32,256]{2,1,0:T(8,128)S(1)}, f32[4,32,256]{2,1,0:T(8,128)}, u32[]{:S(2)}) copy-start(f32[4,32,256]{2,1,0:T(8,128)} %copy-done.2) | copy-start | bytes 393220
  404.8 17.4 %copy-start.16 = (bf16[4,64,256]{2,1,0:T(8,128)(2,1)S(1)}, bf16[4,64,256]{2,1,0:T(8,128)(2,1)}, u32[]{:S(2)}) copy-start(bf16[4,64,256]{2,1,0:T(8,128)(2,1)} %param.20) | copy-start | bytes 393220
Sparse Core Ops, SparseCore 0:
  19.8 73.4 all-reduce.7
  98.4 275.8 all-reduce.9

commit v2 on v0

--- a/solution.py
+++ b/solution.py
@@ -1,7 +1,11 @@
+import functools
+
 import jax
 import jax.numpy as jnp
 from jax import lax
 from jax.sharding import Mesh
+from jax.experimental import pallas as pl
+from jax.experimental.pallas import tpu as pltpu
 from jax.sharding import PartitionSpec as P
 
 highest = lax.Precision.HIGHEST
@@ -50,6 +54,82 @@
         win[None], jnp.reshape(base, (1,)), row[None], jnp.reshape(box & 1, (1,)) == 1,
         level_coupling,
     )[0]
+
+
+def tree_kernel(dev_ref, ftop_ref, fleaf_ref, fpair_ref, top5_ref, ext2_ref, ext0_ref, ext1_ref,
+                rt_ref, ct_ref, cp_ref, cb_ref, near_ref, out_ref,
+                p5, p6, p7, p8, p9, e3, e4, *, starts, k, r, leaves, width, levels):
+    def dot(a, b):
+        return jnp.dot(a, b, precision=highest, preferred_element_type=jnp.float32)
+
+    def halve_rows(x, n, height):
+        v = x.reshape(n // 2, 2 * k, r)
+        even = v[:, :k].reshape(n // 2 * k, r)
+        odd = v[:, k:].reshape(n // 2 * k, r)
+        return dot(even, rt_ref[2 * height]) + dot(odd, rt_ref[2 * height + 1])
+
+    def box(ref, i):
+        return ref[pl.ds(pl.multiple_of(i * k, k), k), :]
+
+    def coupling(ref, start, base, odd, row_at, level):
+        total = jnp.zeros((k, r), jnp.float32)
+        for w, cls in ((0, 1), (1, 2), (4, 4), (5, 5)):
+            hit = jnp.int32(0)
+            for j in range(4):
+                e = row_at(j)
+                hit = hit | ((e == base + w) & (e >= 0)).astype(jnp.int32)
+            scale = hit.astype(jnp.float32)
+            c = cls - odd
+            total = total + dot(box(ref, start + w) * scale, cp_ref[level * 6 + c])
+        return total
+
+    d = dev_ref[0]
+    grp = d >> 3
+    zeros2 = jnp.zeros((2 * k, r), jnp.float32)
+    pads = [p5, p6, p7, p8, p9]
+    x = top5_ref[...]
+    n = x.shape[0] // k
+    for idx, ref in enumerate(pads):
+        ref[pl.ds(0, 2 * k), :] = zeros2
+        ref[pl.ds((n + 2) * k, 2 * k), :] = zeros2
+        ref[pl.ds(2 * k, n * k), :] = x
+        if idx + 1 < len(pads):
+            x = halve_rows(x, n, 5 + idx)
+            n = n // 2
+    e3[...] = halve_rows(ext2_ref[...], 24, 2)
+    e4[...] = halve_rows(e3[...], 12, 3)
+
+    g = {}
+    for height in range(5, levels):
+        t = grp >> (height - 5)
+        base = 2 * (t >> 1) - 2
+        row0 = (starts[height] + t) * 4
+        g[height] = coupling(pads[height - 5], base + 2, base, t & 1,
+                             lambda j, row0=row0: ftop_ref[row0 + j], height)
+    lg = d & 7
+    mids = {2: (ext2_ref, 2 * (lg >> 1) + 6), 3: (e3, 2 * (lg >> 2) + 2), 4: (e4, 0)}
+    for height in range(2, 5):
+        t = d >> (height - 2)
+        base = 2 * (t >> 1) - 2
+        row0 = (starts[height] + t) * 4
+        ref, start = mids[height]
+        g[height] = coupling(ref, start, base, t & 1,
+                             lambda j, row0=row0: ftop_ref[row0 + j], height)
+    expansion = g[levels - 1]
+    for height in range(levels - 2, 1, -1):
+        bit = (d >> (height - 2)) & 1
+        expansion = g[height] + dot(expansion, ct_ref[2 * height + bit])
+    b1 = []
+    for j in range(2):
+        gj = coupling(ext1_ref, 0, 2 * d - 2, j, lambda e, j=j: fpair_ref[j * 4 + e], 1)
+        b1.append(gj + dot(expansion, ct_ref[2 + j]))
+    for i in range(leaves):
+        st = 2 * (i >> 1) + 2
+        gi = coupling(ext0_ref, st, leaves * d + 2 * (i >> 1) - 2, i & 1,
+                      lambda e, i=i: fleaf_ref[i * 4 + e], 0)
+        b0 = gi + dot(b1[i >> 1], ct_ref[i & 1])
+        far = jnp.dot(b0.astype(jnp.bfloat16), cb_ref[i], preferred_element_type=jnp.float32)
+        out_ref[:, pl.ds(i * width, width)] = far + near_ref[i]
 
 
 def local(
@@ -87,14 +167,6 @@
     up_levels = [grp]
     for height in range(2, 5):
         up_levels.append(halve(up_levels[-1], row_transfer[height]))
-    own5 = up_levels[-1]
-    top = [lax.all_gather(own5[0], "yz", axis=0, tiled=False)]
-    for height in range(5, levels_total - 1):
-        top.append(halve(top[-1], row_transfer[height]))
-
-    ext = [padded(grp, "yz", group_size)]
-    for height in range(2, 4):
-        ext.append(halve(ext[-1], row_transfer[height]))
 
     products = jnp.einsum("klp,ljpq->ljkq", points, near_blocks, preferred_element_type=jnp.float32)
     span_width = leaves + 2 * near_reach
@@ -126,49 +198,37 @@
         starts[height] = running
         running = running + (all_leaves >> height)
 
-    def top_row(height, box):
-        return lax.dynamic_index_in_dim(far_top, starts[height] + box, 0, keepdims=False)
-
-    g = {}
-    for height in range(5, levels_total):
-        arr = top[height - 5]
-        arr = jnp.pad(arr, ((2, 2), (0, 0), (0, 0)))
-        box = group >> (height - 5)
-        g[height] = one_box(arr, -2, box, top_row(height, box), coupling[height])
-    for height in range(2, 5):
-        arr = ext[height - 2]
-        box = device >> (height - 2)
-        offset = (group - 1) * (group_size >> (height - 2))
-        g[height] = one_box(arr, offset, box, top_row(height, box), coupling[height])
-
-    expansion = g[levels_total - 1]
-    for height in range(levels_total - 2, 1, -1):
-        box = device >> (height - 2)
-        matrix = lax.dynamic_index_in_dim(col_transfer[height], box & 1, 0, keepdims=False)
-        expansion = g[height] + jnp.dot(expansion, matrix, precision=highest)
-
-    odd1 = jnp.array([False, True])
-    bases1 = jnp.full((2,), 2 * device - 2, jnp.int32)
-    win1 = jnp.stack([ext1[0:6], ext1[0:6]], axis=0)
-    g1 = window_coupling(win1, bases1, far_pair, odd1, coupling[1])
-    b1 = jnp.einsum("kr,jrs->jks", expansion, col_transfer[1], precision=highest) + g1
-
-    odd0 = jnp.array([False, True, False, True])
-    local_starts = (2, 2, 4, 4)
-    bases0 = first_leaf + jnp.array([0, 0, 2, 2], jnp.int32) - 2
-    win0 = jnp.stack([ext0[s : s + 6] for s in local_starts], axis=0)
-    g0 = window_coupling(win0, bases0, far_leaf, odd0, coupling[0])
-    pushed = jnp.einsum("jkr,crs->jcks", b1, col_transfer[0], precision=highest)
-    b0 = pushed.reshape(leaves, probe_count, basis_rank) + g0
-
-    far_field = jnp.einsum(
-        "lkr,lrp->klp",
-        b0.astype(jnp.bfloat16),
+    gathered = lax.all_gather(up_levels[-1][0], "yz", axis=0, tiled=False)
+    ext2 = padded(grp, "yz", group_size)
+    k, r = probe_count, basis_rank
+    flat = lambda x: x.reshape(-1, r)
+    n5 = gathered.shape[0]
+    smem = pl.BlockSpec(memory_space=pltpu.SMEM)
+    vmem = pl.BlockSpec(memory_space=pltpu.VMEM)
+    out = pl.pallas_call(
+        functools.partial(tree_kernel, starts=starts, k=k, r=r, leaves=leaves,
+                          width=leaf_width, levels=levels_total),
+        out_shape=jax.ShapeDtypeStruct((probe_count, leaves * leaf_width), jnp.float32),
+        in_specs=[smem] * 4 + [vmem] * 9,
+        out_specs=vmem,
+        scratch_shapes=[pltpu.VMEM(((n5 >> i) * k + 4 * k, r), jnp.float32) for i in range(5)]
+        + [pltpu.VMEM((12 * k, r), jnp.float32), pltpu.VMEM((6 * k, r), jnp.float32)],
+    )(
+        jnp.reshape(device, (1,)).astype(jnp.int32),
+        far_top.reshape(-1),
+        far_leaf.reshape(-1),
+        far_pair.reshape(-1),
+        flat(gathered),
+        flat(ext2),
+        flat(ext0),
+        flat(ext1),
+        row_transfer.reshape(-1, r, r),
+        col_transfer.reshape(-1, r, r),
+        coupling.reshape(-1, r, r),
         col_basis,
-        preferred_element_type=jnp.float32,
-    )
-    own_near_t = jnp.transpose(own_near, (1, 0, 2))
-    return (far_field + own_near_t).reshape(probe_count, leaves * leaf_width)
+        own_near,
+    )
+    return out
 
 
 def solution(mesh):

time: 185 us -> 144 us (0.78)
  other arithmetic: 39.1 us -> 6.03 us
  matrix products: 23.8 us -> 8.41 us
  Pallas kernels: 0 us -> 10.9 us
  local copies, waits for them, and re-layouts: 12.9 us -> 9.37 us
  starting transfers between devices: 29.4 us -> 31.4 us
    squeeze x6 -> x0, other arithmetic: 15.8 us -> none  [the longest x2 8.34 us: window_coupling(): level_coupling[odd_cls[i]]]
    select_n x5 -> x0, other arithmetic: 14.9 us -> none  [window_coupling(): mats.append(jnp.where(hits[i][:, None, None], chosen, 0.0))]
    pallas_call x0 -> x1, Pallas kernels: none -> 10.9 us  [local(): pl.pallas_call(functools.partial(tree_kernel, starts=starts, k=k, r=r, le...]
    dot_general x11 -> x5, matrix products: 14.1 us -> 5.4 us  [halve(): return jnp.einsum('bjkr,jrs->bks', paired, transfer, precision=highest)]
    dot_general x20 -> x0, matrix products: 6.69 us -> none  [the longest x10 3.47 us: window_coupling(): return jnp.einsum('bkr,brs->bks', stacked, matrix, precision=highest)]
    reduce_or x5 -> x0, other arithmetic: 3.22 us -> none  [window_coupling(): jnp.any((rows == (bases + w)[:, None]) & (rows >= 0), axis=1)]
    squeeze x8 -> x0, local copies, waits for them, and re-layouts: 3.17 us -> none  [window_coupling(): stacked = jnp.concatenate([windows[:, w] for w in picks], axis=-1)]
    ppermute x3, starting transfers between devices: 20 us -> 22.9 us  [padded(): after = lax.ppermute(shard[:width], axis, down)]
  transfers between devices with their start and end apart: 6 -> 6, of which waited for: 0 -> 0; matrix products, arithmetic and copies ran while one was open for 39% -> 14% of each run, Pallas kernels for 0% -> 0%
where the time goes in v2:
time: 144 us; the launch traced here: 143 us
  blocking collectives  76.9 us (53%)
  starting transfers between devices  31.4 us (22%)
  Pallas kernels  10.9 us (8%)
  local copies, waits for them, and re-layouts  9.37 us (7%)
  matrix products  8.41 us (6%)
  other arithmetic  6.03 us (4%)
    all_gather x1, blocking collectives, local(): gathered = lax.all_gather(up_levels[-1][0], 'yz', axis=0, tiled=False)  50.3 us
    all_gather x1, blocking collectives, local(): grp = lax.all_gather(a2[0], GROUP, axis=0, tiled=False)  26.6 us
    ppermute x3, starting transfers between devices, padded(): after = lax.ppermute(shard[:width], axis, down)  22.9 us
    pallas_call x1, Pallas kernels, local(): pl.pallas_call(functools.partial(tree_kernel, starts=starts, k=k, r=r, le...  10.9 us
    ppermute x3, starting transfers between devices, padded(): before = lax.ppermute(shard[length - width:], axis, up)  8.48 us
    dot_general x5, matrix products, halve(): return jnp.einsum('bjkr,jrs->bks', paired, transfer, precision=highest)  5.4 us
  transfers between devices with their start and end apart: 6, of which 0 were waited for; matrix products, arithmetic and copies ran while one was open for 14% of the time, Pallas kernels for 0%

profile of v2, /device:TPU:1, one launch (start us, length us, event | category | flops | bytes accessed | tf_op | source)
XLA Modules:
  0.0 143.2 jit_solution(15501204503798089590)
XLA Ops:
  0.0 1.2 fusion.2
  1.2 1.1 convolution_bitcast_fusion.3
  2.3 0.7 pad_maximum_fusion.2
  3.0 5.8 %collective-permute-start.3 = (f32[6,32,64]{2,1,0:T(8,128)}, f32[6,32,64]{2,1,0:T(8,128)}, u32[]{:S(2)}, u32[]{:S(2)}) collective-permute-start(f32[6,32,64]{2,1,0:T(8,128)} %pad_maximum_fusion.2), channel_id=1, source_target_pairs={{1,0},{2,1},{3,2},{4,3},{5,4},{6,5},{7,6},{8,7},{9,8},{10,9},{11,1... | collective-permute-start | bytes 147464 | tf_op jit(solution)/shard_map/ppermute | solution.py:21
  8.7 1.9 %collective-permute-start.2 = (f32[6,32,64]{2,1,0:T(8,128)}, f32[6,32,64]{2,1,0:T(8,128)}, u32[]{:S(2)}, u32[]{:S(2)}) collective-permute-start(f32[6,32,64]{2,1,0:T(8,128)} %pad_maximum_fusion.2), channel_id=1, source_target_pairs={{0,1},{1,2},{2,3},{3,4},{4,5},{5,6},{6,7},{7,8},{8,9},{9,10},{10,1... | collective-permute-start | bytes 147464 | tf_op jit(solution)/shard_map/ppermute | solution.py:20
  10.7 1.1 convolution_bitcast_fusion.5
  11.7 26.6 %all-gather = f32[256,64]{1,0:T(8,128)S(1)} all-gather(f32[32,64]{1,0:T(8,128)S(1)} %convolution_bitcast_fusion.5), channel_id=2, replica_groups=mesh['yz'=64,'core'=2,'sub'=4] {'core','sub'}, dimensions={0}, use_global_device_ids=true | all-gather | bytes 73728 | tf_op jit(solution)/shard_map/all_gather | solution.py:166
  38.4 1.3 collective-permute-start.1
  39.6 4.7 %collective-permute-start = (f32[8,32,64]{2,1,0:T(8,128)S(1)}, f32[8,32,64]{2,1,0:T(8,128)}, u32[]{:S(2)}, u32[]{:S(2)}) collective-permute-start(f32[8,32,64]{2,1,0:T(8,128)S(1)} %bitcast.72), channel_id=1, source_target_pairs={{0,8},{8,16},{16,24},{24,32},{32,40},{40,48},{48,56},{56,64},{64,7... | collective-permute-start | bytes 196616 | tf_op jit(solution)/shard_map/ppermute | solution.py:20
  44.3 0.9 reshape.140
  45.2 0.7 broadcast_compare_fusion
  45.9 0.7 broadcast_subtract_fusion
  47.1 1.2 convolution_bitcast_fusion
  48.4 0.7 fusion.24
  49.7 1.9 %collective-permute-start.4 = (f32[2,32,256]{2,1,0:T(8,128)}, f32[2,32,256]{2,1,0:T(8,128)}, u32[]{:S(2)}, u32[]{:S(2)}) collective-permute-start(f32[2,32,256]{2,1,0:T(8,128)} %copy.32), channel_id=1, source_target_pairs={{0,1},{1,2},{2,3},{3,4},{4,5},{5,6},{6,7},{7,8},{8,9},{9,10},{10,1... | collective-permute-start | bytes 196616 | tf_op jit(solution)/shard_map/ppermute | solution.py:20
  51.6 1.1 convolution_bitcast_fusion.1
  52.8 1.1 convolution_bitcast_fusion.2
  53.8 1.1 convolution_bitcast_fusion.4
  54.9 50.3 %all-gather.1.top5_ref = f32[2048,64]{1,0:T(8,128)} all-gather(f32[32,64]{1,0:T(8,128)S(1)} %convolution_bitcast_fusion.4), channel_id=3, replica_groups=mesh['yz'=64,'core'=2,'sub'=4] {'yz'}, dimensions={0}, use_global_device_ids=true | all-gather | bytes 532480 | tf_op jit(solution)/shard_map/all_gather | solution.py:201
  105.2 0.7 reshape.116.fleaf_ref
  105.9 0.7 reshape.117.fpair_ref
  106.8 0.9 reshape.115.ftop_ref
  107.6 0.8 copy.33
  108.5 15.9 %collective-permute-start.5 = (f32[2,32,256]{2,1,0:T(8,128)S(1)}, f32[2,32,256]{2,1,0:T(8,128)S(1)}, u32[]{:S(2)}, u32[]{:S(2)}) collective-permute-start(f32[2,32,256]{2,1,0:T(8,128)S(1)} %copy.33), channel_id=1, source_target_pairs={{1,0},{2,1},{3,2},{4,3},{5,4},{6,5},{7,6},{8,7},{9,8},{10,9},{11,1... | collective-permute-start | bytes 196616 | tf_op jit(solution)/shard_map/ppermute | solution.py:21
  124.4 0.8 slice.100
  125.3 0.8 slice.99
  126.1 0.7 pad_maximum_fusion.1
  126.8 0.8 slice.102
  127.6 0.8 slice.101
  129.0 0.9 fusion.6
  129.9 1.8 %pad_maximum_fusion = f32[24,32,64]{2,1,0:T(8,128)} fusion(f32[8,32,64]{2,1,0:T(8,128)} %collective-permute-done.1, f32[8,32,64]{2,1,0:T(8,128)S(1)} %bitcast.74, f32[8,32,64]{2,1,0:T(8,128)} %collective-permute-done), kind=kLoop, calls=%fused_computation.8 | loop fusion | flops 98304 | bytes 393216 | tf_op jit(solution)/shard_map/concatenate | solution.py:22
  132.3 10.9 %shard_map.109 = f32[32,1024]{1,0:T(8,128)} custom-call(s32[1]{0:T(128)} %bitcast.dev_ref, s32[4080]{0:T(1024)} %reshape.115.ftop_ref, s32[16]{0:T(128)} %reshape.116.fleaf_ref, s32[8]{0:T(128)} %reshape.117.fpair_ref, f32[2048,64]{1,0:T(8,128)} %all-gather.1.top5_ref, f32[768,64]{1,0:T(8,128)} %bitcast.69, f32[384,64]{1,0:T(8,128)} %bitcast.76, ...), custom_call_target="tpu_custom_call" | custom-call | tf_op jit(solution)/shard_map/pallas_call | solution.py:208
  (23 shorter events, 2.8 us)
Async XLA Ops:
  0.0 46.6 %copy-start = (bf16[4,5,256,256]{3,2,1,0:T(8,128)(2,1)S(1)}, bf16[4,5,256,256]{3,2,1,0:T(8,128)(2,1)}, u32[]{:S(2)}) copy-start(bf16[4,5,256,256]{3,2,1,0:T(8,128)(2,1)} %param.18) | copy-start | bytes 7864324
  3.0 105.5 %collective-permute-start.3 = (f32[6,32,64]{2,1,0:T(8,128)}, f32[6,32,64]{2,1,0:T(8,128)}, u32[]{:S(2)}, u32[]{:S(2)}) collective-permute-start(f32[6,32,64]{2,1,0:T(8,128)} %pad_maximum_fusion.2), channel_id=1, source_target_pairs={{1,0},{2,1},{3,2},{4,3},{5,4},{6,5},{7,6},{8,7},{9,8},{10,9},{11,1... | collective-permute-start | bytes 147464 | tf_op jit(solution)/shard_map/ppermute | solution.py:21
  8.7 116.5 %collective-permute-start.2 = (f32[6,32,64]{2,1,0:T(8,128)}, f32[6,32,64]{2,1,0:T(8,128)}, u32[]{:S(2)}, u32[]{:S(2)}) collective-permute-start(f32[6,32,64]{2,1,0:T(8,128)} %pad_maximum_fusion.2), channel_id=1, source_target_pairs={{0,1},{1,2},{2,3},{3,4},{4,5},{5,6},{6,7},{7,8},{8,9},{9,10},{10,1... | collective-permute-start | bytes 147464 | tf_op jit(solution)/shard_map/ppermute | solution.py:20
  38.4 91.5 %collective-permute-start.1 = (f32[8,32,64]{2,1,0:T(8,128)S(1)}, f32[8,32,64]{2,1,0:T(8,128)}, u32[]{:S(2)}, u32[]{:S(2)}) collective-permute-start(f32[8,32,64]{2,1,0:T(8,128)S(1)} %bitcast.71), channel_id=1, source_target_pairs={{8,0},{16,8},{24,16},{32,24},{40,32},{48,40},{56,48},{64,56},{72,6... | collective-permute-start | bytes 196616 | tf_op jit(solution)/shard_map/ppermute | solution.py:21
  39.6 90.2 %collective-permute-start = (f32[8,32,64]{2,1,0:T(8,128)S(1)}, f32[8,32,64]{2,1,0:T(8,128)}, u32[]{:S(2)}, u32[]{:S(2)}) collective-permute-start(f32[8,32,64]{2,1,0:T(8,128)S(1)} %bitcast.72), channel_id=1, source_target_pairs={{0,8},{8,16},{16,24},{24,32},{32,40},{40,48},{48,56},{56,64},{64,7... | collective-permute-start | bytes 196616 | tf_op jit(solution)/shard_map/ppermute | solution.py:20
  47.1 58.1 %copy-start.3 = (s32[4,4]{1,0:T(4,128)S(1)}, s32[4,4]{1,0:T(4,128)}, u32[]{:S(2)}) copy-start(s32[4,4]{1,0:T(4,128)} %param.20) | copy-start | bytes 196
  47.1 58.8 %copy-start.4 = (s32[2,4]{1,0:T(2,128)S(1)}, s32[2,4]{1,0:T(2,128)}, u32[]{:S(2)}) copy-start(s32[2,4]{1,0:T(2,128)} %param.21) | copy-start | bytes 100
  47.1 59.4 %copy-start.2 = (s32[1020,4]{0,1:T(4,128)S(1)}, s32[1020,4]{0,1:T(4,128)}, u32[]{:S(2)}) copy-start(s32[1020,4]{0,1:T(4,128)} %param.22) | copy-start | bytes 48964
  49.7 79.3 %collective-permute-start.4 = (f32[2,32,256]{2,1,0:T(8,128)}, f32[2,32,256]{2,1,0:T(8,128)}, u32[]{:S(2)}, u32[]{:S(2)}) collective-permute-start(f32[2,32,256]{2,1,0:T(8,128)} %copy.32), channel_id=1, source_target_pairs={{0,1},{1,2},{2,3},{3,4},{4,5},{5,6},{6,7},{7,8},{8,9},{9,10},{10,1... | collective-permute-start | bytes 196616 | tf_op jit(solution)/shard_map/ppermute | solution.py:20
  108.5 23.1 %collective-permute-start.5 = (f32[2,32,256]{2,1,0:T(8,128)S(1)}, f32[2,32,256]{2,1,0:T(8,128)S(1)}, u32[]{:S(2)}, u32[]{:S(2)}) collective-permute-start(f32[2,32,256]{2,1,0:T(8,128)S(1)} %copy.33), channel_id=1, source_target_pairs={{1,0},{2,1},{3,2},{4,3},{5,4},{6,5},{7,6},{8,7},{9,8},{10,9},{11,1... | collective-permute-start | bytes 196616 | tf_op jit(solution)/shard_map/ppermute | solution.py:21
  131.7 0.6 copy-start.1

commit v3 on v2

--- a/solution.py
+++ b/solution.py
@@ -19,7 +19,7 @@
     down = [(j, i) for i, j in up]
     before = lax.ppermute(shard[length - width :], axis, up)
     after = lax.ppermute(shard[:width], axis, down)
-    return jnp.concatenate([before, shard, after], axis=0)
+    return before, after
 
 
 def halve(coefficients, transfer):
@@ -56,9 +56,10 @@
     )[0]
 
 
-def tree_kernel(dev_ref, ftop_ref, fleaf_ref, fpair_ref, top5_ref, ext2_ref, ext0_ref, ext1_ref,
-                rt_ref, ct_ref, cp_ref, cb_ref, near_ref, out_ref,
-                p5, p6, p7, p8, p9, e3, e4, *, starts, k, r, leaves, width, levels):
+def tree_kernel(dev_ref, ftop_ref, fleaf_ref, fpair_ref, top5_ref, gb_ref, gown_ref, ga_ref,
+                pb_ref, pown_ref, pa_ref, rt_ref, ct_ref, cp_ref, cb_ref, spread_ref, rb_ref, ra_ref,
+                out_ref, p5, p6, p7, p8, p9, ext2_ref, e3, e4, *, starts, k, r, leaves, width, levels,
+                reach):
     def dot(a, b):
         return jnp.dot(a, b, precision=highest, preferred_element_type=jnp.float32)
 
@@ -71,7 +72,7 @@
     def box(ref, i):
         return ref[pl.ds(pl.multiple_of(i * k, k), k), :]
 
-    def coupling(ref, start, base, odd, row_at, level):
+    def coupling(get, base, odd, row_at, level):
         total = jnp.zeros((k, r), jnp.float32)
         for w, cls in ((0, 1), (1, 2), (4, 4), (5, 5)):
             hit = jnp.int32(0)
@@ -80,7 +81,7 @@
                 hit = hit | ((e == base + w) & (e >= 0)).astype(jnp.int32)
             scale = hit.astype(jnp.float32)
             c = cls - odd
-            total = total + dot(box(ref, start + w) * scale, cp_ref[level * 6 + c])
+            total = total + dot(get(w) * scale, cp_ref[level * 6 + c])
         return total
 
     d = dev_ref[0]
@@ -96,6 +97,10 @@
         if idx + 1 < len(pads):
             x = halve_rows(x, n, 5 + idx)
             n = n // 2
+    span = gown_ref.shape[0]
+    ext2_ref[pl.ds(0, span), :] = gb_ref[...]
+    ext2_ref[pl.ds(span, span), :] = gown_ref[...]
+    ext2_ref[pl.ds(2 * span, span), :] = ga_ref[...]
     e3[...] = halve_rows(ext2_ref[...], 24, 2)
     e4[...] = halve_rows(e3[...], 12, 3)
 
@@ -103,33 +108,52 @@
     for height in range(5, levels):
         t = grp >> (height - 5)
         base = 2 * (t >> 1) - 2
-        row0 = (starts[height] + t) * 4
-        g[height] = coupling(pads[height - 5], base + 2, base, t & 1,
-                             lambda j, row0=row0: ftop_ref[row0 + j], height)
+        row0 = starts[height] + t
+        g[height] = coupling(lambda w, ref=pads[height - 5], st=base + 2: box(ref, st + w),
+                             base, t & 1, lambda j, row=row0: ftop_ref[row, j], height)
     lg = d & 7
     mids = {2: (ext2_ref, 2 * (lg >> 1) + 6), 3: (e3, 2 * (lg >> 2) + 2), 4: (e4, 0)}
     for height in range(2, 5):
         t = d >> (height - 2)
         base = 2 * (t >> 1) - 2
-        row0 = (starts[height] + t) * 4
+        row0 = starts[height] + t
         ref, start = mids[height]
-        g[height] = coupling(ref, start, base, t & 1,
-                             lambda j, row0=row0: ftop_ref[row0 + j], height)
+        g[height] = coupling(lambda w, ref=ref, st=start: box(ref, st + w),
+                             base, t & 1, lambda j, row=row0: ftop_ref[row, j], height)
     expansion = g[levels - 1]
     for height in range(levels - 2, 1, -1):
         bit = (d >> (height - 2)) & 1
         expansion = g[height] + dot(expansion, ct_ref[2 * height + bit])
+    rows_pack = pown_ref.shape[0] // k
+
+    def pack_box(e):
+        ref = (pb_ref, pown_ref, pa_ref)[e // rows_pack]
+        return box(ref, e % rows_pack)
+
+    level1 = rows_pack - leaves
+
+    def ext1_box(e):
+        return pack_box((e // level1) * rows_pack + leaves + e % level1)
+
+    def ext0_box(e):
+        return pack_box((e // leaves) * rows_pack + e % leaves)
+
     b1 = []
     for j in range(2):
-        gj = coupling(ext1_ref, 0, 2 * d - 2, j, lambda e, j=j: fpair_ref[j * 4 + e], 1)
+        gj = coupling(ext1_box, 2 * d - 2, j, lambda e, j=j: fpair_ref[j, e], 1)
         b1.append(gj + dot(expansion, ct_ref[2 + j]))
     for i in range(leaves):
         st = 2 * (i >> 1) + 2
-        gi = coupling(ext0_ref, st, leaves * d + 2 * (i >> 1) - 2, i & 1,
-                      lambda e, i=i: fleaf_ref[i * 4 + e], 0)
+        gi = coupling(lambda w, st=st: ext0_box(st + w), leaves * d + 2 * (i >> 1) - 2, i & 1,
+                      lambda e, i=i: fleaf_ref[i, e], 0)
         b0 = gi + dot(b1[i >> 1], ct_ref[i & 1])
         far = jnp.dot(b0.astype(jnp.bfloat16), cb_ref[i], preferred_element_type=jnp.float32)
-        out_ref[:, pl.ds(i * width, width)] = far + near_ref[i]
+        near = spread_ref[reach + i]
+        if i < reach:
+            near = near + rb_ref[i]
+        if i >= leaves - reach:
+            near = near + ra_ref[i - (leaves - reach)]
+        out_ref[:, pl.ds(i * width, width)] = far + near
 
 
 def local(
@@ -177,20 +201,10 @@
     ).astype(jnp.float32)
     spread = jnp.einsum("lje,ljkq->ekq", scatter_table, products, precision=highest)
     rims = jnp.concatenate([spread[:near_reach], spread[span_width - near_reach :]], axis=0)
-    rim_ext = padded(rims, ALL, near_reach)
-    own_near = spread[near_reach : near_reach + leaves]
-    own_near = own_near.at[:near_reach].add(rim_ext[:near_reach])
-    own_near = own_near.at[leaves - near_reach :].add(rim_ext[3 * near_reach :])
+    rim_before, rim_after = padded(rims, ALL, near_reach)
 
     packed = jnp.concatenate([a0, a1], axis=0)
-    pack_ext = padded(packed, ALL, packed.shape[0])
-    rows_pack = packed.shape[0]
-    ext0 = jnp.concatenate(
-        [pack_ext[:leaves], a0, pack_ext[rows_pack + rows_pack : rows_pack * 2 + leaves]], axis=0
-    )
-    ext1 = jnp.concatenate(
-        [pack_ext[leaves:rows_pack], a1, pack_ext[rows_pack * 2 + leaves :]], axis=0
-    )
+    pack_before, pack_after = padded(packed, ALL, packed.shape[0])
 
     starts = {}
     running = 0
@@ -199,7 +213,7 @@
         running = running + (all_leaves >> height)
 
     gathered = lax.all_gather(up_levels[-1][0], "yz", axis=0, tiled=False)
-    ext2 = padded(grp, "yz", group_size)
+    grp_before, grp_after = padded(grp, "yz", group_size)
     k, r = probe_count, basis_rank
     flat = lambda x: x.reshape(-1, r)
     n5 = gathered.shape[0]
@@ -207,26 +221,32 @@
     vmem = pl.BlockSpec(memory_space=pltpu.VMEM)
     out = pl.pallas_call(
         functools.partial(tree_kernel, starts=starts, k=k, r=r, leaves=leaves,
-                          width=leaf_width, levels=levels_total),
+                          width=leaf_width, levels=levels_total, reach=near_reach),
         out_shape=jax.ShapeDtypeStruct((probe_count, leaves * leaf_width), jnp.float32),
-        in_specs=[smem] * 4 + [vmem] * 9,
+        in_specs=[smem] * 4 + [vmem] * 14,
         out_specs=vmem,
         scratch_shapes=[pltpu.VMEM(((n5 >> i) * k + 4 * k, r), jnp.float32) for i in range(5)]
-        + [pltpu.VMEM((12 * k, r), jnp.float32), pltpu.VMEM((6 * k, r), jnp.float32)],
+        + [pltpu.VMEM((3 * group_size * k, r), jnp.float32),
+           pltpu.VMEM((12 * k, r), jnp.float32), pltpu.VMEM((6 * k, r), jnp.float32)],
     )(
         jnp.reshape(device, (1,)).astype(jnp.int32),
-        far_top.reshape(-1),
-        far_leaf.reshape(-1),
-        far_pair.reshape(-1),
+        far_top,
+        far_leaf,
+        far_pair,
         flat(gathered),
-        flat(ext2),
-        flat(ext0),
-        flat(ext1),
+        flat(grp_before),
+        flat(grp),
+        flat(grp_after),
+        flat(pack_before),
+        flat(packed),
+        flat(pack_after),
         row_transfer.reshape(-1, r, r),
         col_transfer.reshape(-1, r, r),
         coupling.reshape(-1, r, r),
         col_basis,
-        own_near,
+        spread,
+        rim_before,
+        rim_after,
     )
     return out
 

time: 144 us -> 138 us (0.958)
  the two profiles are of different devices: /device:TPU:1 before, /device:TPU:6 now
where the time goes in v3:
time: 138 us; the launch traced here: 137 us
  blocking collectives  88.9 us (64%)
  Pallas kernels  17.9 us (13%)
  starting transfers between devices  17.2 us (12%)
  matrix products  8.42 us (6%)
  local copies, waits for them, and re-layouts  3.41 us (2%)
    all_gather x1, blocking collectives, local(): gathered = lax.all_gather(up_levels[-1][0], 'yz', axis=0, tiled=False)  65.2 us
    all_gather x1, blocking collectives, local(): grp = lax.all_gather(a2[0], GROUP, axis=0, tiled=False)  23.7 us
    pallas_call x1, Pallas kernels, local(): pl.pallas_call(functools.partial(tree_kernel, starts=starts, k=k, r=r, le...  17.9 us
    ppermute x3, starting transfers between devices, padded(): before = lax.ppermute(shard[length - width:], axis, up)  9.45 us
    ppermute x3, starting transfers between devices, padded(): after = lax.ppermute(shard[:width], axis, down)  7.75 us
    dot_general x5, matrix products, halve(): return jnp.einsum('bjkr,jrs->bks', paired, transfer, precision=highest)  5.41 us
  transfers between devices with their start and end apart: 6, of which 0 were waited for; matrix products, arithmetic and copies ran while one was open for 7% of the time, Pallas kernels for 0%

profile of v3, /device:TPU:6, one launch (start us, length us, event | category | flops | bytes accessed | tf_op | source)
XLA Modules:
  0.0 137.4 jit_solution(4983661780713273881)
XLA Ops:
  0.0 1.2 fusion.2
  1.2 1.1 convolution_bitcast_fusion.3
  2.4 2.7 %collective-permute-start.3 = (f32[6,32,64]{2,1,0:T(8,128)S(1)}, f32[6,32,64]{2,1,0:T(8,128)S(1)}, u32[]{:S(2)}, u32[]{:S(2)}) collective-permute-start(f32[6,32,64]{2,1,0:T(8,128)S(1)} %pad_maximum_fusion), channel_id=1, source_target_pairs={{1,0},{2,1},{3,2},{4,3},{5,4},{6,5},{7,6},{8,7},{9,8},{10,9},{11,1... | collective-permute-start | bytes 147464 | tf_op jit(solution)/shard_map/ppermute | solution.py:21
  5.1 4.0 %collective-permute-start.2 = (f32[6,32,64]{2,1,0:T(8,128)S(1)}, f32[6,32,64]{2,1,0:T(8,128)}, u32[]{:S(2)}, u32[]{:S(2)}) collective-permute-start(f32[6,32,64]{2,1,0:T(8,128)S(1)} %pad_maximum_fusion), channel_id=1, source_target_pairs={{0,1},{1,2},{2,3},{3,4},{4,5},{5,6},{6,7},{7,8},{8,9},{9,10},{10,1... | collective-permute-start | bytes 147464 | tf_op jit(solution)/shard_map/ppermute | solution.py:20
  9.2 1.1 convolution_bitcast_fusion.5
  10.2 23.7 %all-gather.gown_ref = f32[256,64]{1,0:T(8,128)S(1)} all-gather(f32[32,64]{1,0:T(8,128)S(1)} %convolution_bitcast_fusion.5), channel_id=2, replica_groups=mesh['yz'=64,'core'=2,'sub'=4] {'core','sub'}, dimensions={0}, use_global_device_ids=true | all-gather | bytes 73728 | tf_op jit(solution)/shard_map/all_gather | solution.py:190
  33.9 2.4 %collective-permute-start = (f32[8,32,64]{2,1,0:T(8,128)S(1)}, f32[8,32,64]{2,1,0:T(8,128)S(1)}, u32[]{:S(2)}, u32[]{:S(2)}) collective-permute-start(f32[8,32,64]{2,1,0:T(8,128)S(1)} %bitcast.72), channel_id=1, source_target_pairs={{0,8},{8,16},{16,24},{24,32},{32,40},{40,48},{48,56},{56,64},{64,7... | collective-permute-start | bytes 196616 | tf_op jit(solution)/shard_map/ppermute | solution.py:20
  36.3 1.3 collective-permute-start.1
  37.6 0.9 reshape.81
  38.5 0.7 broadcast_compare_fusion
  39.2 0.7 broadcast_subtract_fusion
  39.9 0.5 fusion.10
  40.4 1.3 convolution_bitcast_fusion
  41.7 0.1 copy.16.spread_ref
  41.8 0.7 fusion.22
  42.5 3.7 %collective-permute-start.5 = (f32[2,32,256]{2,1,0:T(8,128)}, f32[2,32,256]{2,1,0:T(8,128)S(1)}, u32[]{:S(2)}, u32[]{:S(2)}) collective-permute-start(f32[2,32,256]{2,1,0:T(8,128)} %get-tuple-element.5), channel_id=1, source_target_pairs={{1,0},{2,1},{3,2},{4,3},{5,4},{6,5},{7,6},{8,7},{9,8},{10,9},{11,1... | collective-permute-start | bytes 196616 | tf_op jit(solution)/shard_map/ppermute | solution.py:21
  46.2 1.1 convolution_bitcast_fusion.1
  47.4 1.1 convolution_bitcast_fusion.2
  48.4 1.1 convolution_bitcast_fusion.4
  49.5 0.0 collective-permute-done.3
  49.5 3.0 %collective-permute-start.4 = (f32[2,32,256]{2,1,0:T(8,128)}, f32[2,32,256]{2,1,0:T(8,128)}, u32[]{:S(2)}, u32[]{:S(2)}) collective-permute-start(f32[2,32,256]{2,1,0:T(8,128)} %get-tuple-element.6), channel_id=1, source_target_pairs={{0,1},{1,2},{2,3},{3,4},{4,5},{5,6},{6,7},{7,8},{8,9},{9,10},{10,1... | collective-permute-start | bytes 196616 | tf_op jit(solution)/shard_map/ppermute | solution.py:20
  52.6 65.2 %all-gather.1.top5_ref = f32[2048,64]{1,0:T(8,128)} all-gather(f32[32,64]{1,0:T(8,128)S(1)} %convolution_bitcast_fusion.4), channel_id=3, replica_groups=mesh['yz'=64,'core'=2,'sub'=4] {'yz'}, dimensions={0}, use_global_device_ids=true | all-gather | bytes 532480 | tf_op jit(solution)/shard_map/all_gather | solution.py:215
  117.8 1.1 copy.15.ftop_ref
  118.8 0.0 collective-permute-done.2
  118.8 0.0 collective-permute-done
  118.8 0.0 collective-permute-done.1
  118.9 0.0 collective-permute-done.5.ra_ref
  118.9 0.0 collective-permute-done.4.rb_ref
  118.9 0.6 copy-done.4
  119.5 0.0 copy-done.5
  119.5 0.0 copy-done.7
  119.6 17.9 %shard_map.109 = f32[32,1024]{1,0:T(8,128)} custom-call(s32[1]{0:T(128)} %bitcast.dev_ref, s32[1020,4]{1,0:T(8,128)} %copy.15.ftop_ref, s32[4,4]{1,0:T(4,128)} %fleaf_ref.1, s32[2,4]{1,0:T(2,128)} %fpair_ref.1, f32[2048,64]{1,0:T(8,128)} %all-gather.1.top5_ref, f32[256,64]{1,0:T(8,128)} %bitcast.79, f32[256,64]{1,0:T(8,128)} %copy-done.2, ...), custom_call_target="tpu_custom_call" | custom-call | tf_op jit(solution)/shard_map/pallas_call | solution.py:222
  (16 shorter events, 0.0 us)
Async XLA Ops:
  0.0 39.9 %copy-start = (bf16[4,5,256,256]{3,2,1,0:T(8,128)(2,1)S(1)}, bf16[4,5,256,256]{3,2,1,0:T(8,128)(2,1)}, u32[]{:S(2)}) copy-start(bf16[4,5,256,256]{3,2,1,0:T(8,128)(2,1)} %param.14) | copy-start | bytes 7864324
  2.4 39.4 %copy-start.3 = (f32[6,32,64]{2,1,0:T(8,128)}, f32[6,32,64]{2,1,0:T(8,128)S(1)}, u32[]{:S(2)}) copy-start(f32[6,32,64]{2,1,0:T(8,128)S(1)} %pad_maximum_fusion) | copy-start | bytes 147460
  2.4 47.1 %collective-permute-start.3 = (f32[6,32,64]{2,1,0:T(8,128)S(1)}, f32[6,32,64]{2,1,0:T(8,128)S(1)}, u32[]{:S(2)}, u32[]{:S(2)}) collective-permute-start(f32[6,32,64]{2,1,0:T(8,128)S(1)} %pad_maximum_fusion), channel_id=1, source_target_pairs={{1,0},{2,1},{3,2},{4,3},{5,4},{6,5},{7,6},{8,7},{9,8},{10,9},{11,1... | collective-permute-start | bytes 147464 | tf_op jit(solution)/shard_map/ppermute | solution.py:21
  5.1 113.7 %collective-permute-start.2 = (f32[6,32,64]{2,1,0:T(8,128)S(1)}, f32[6,32,64]{2,1,0:T(8,128)}, u32[]{:S(2)}, u32[]{:S(2)}) collective-permute-start(f32[6,32,64]{2,1,0:T(8,128)S(1)} %pad_maximum_fusion), channel_id=1, source_target_pairs={{0,1},{1,2},{2,3},{3,4},{4,5},{5,6},{6,7},{7,8},{8,9},{9,10},{10,1... | collective-permute-start | bytes 147464 | tf_op jit(solution)/shard_map/ppermute | solution.py:20
  33.9 12.3 %copy-start.2 = (f32[256,64]{1,0:T(8,128)}, f32[256,64]{1,0:T(8,128)S(1)}, u32[]{:S(2)}) copy-start(f32[256,64]{1,0:T(8,128)S(1)} %all-gather.gown_ref) | copy-start | bytes 196612
  33.9 84.9 %collective-permute-start = (f32[8,32,64]{2,1,0:T(8,128)S(1)}, f32[8,32,64]{2,1,0:T(8,128)S(1)}, u32[]{:S(2)}, u32[]{:S(2)}) collective-permute-start(f32[8,32,64]{2,1,0:T(8,128)S(1)} %bitcast.72), channel_id=1, source_target_pairs={{0,8},{8,16},{16,24},{24,32},{32,40},{40,48},{48,56},{56,64},{64,7... | collective-permute-start | bytes 196616 | tf_op jit(solution)/shard_map/ppermute | solution.py:20
  36.3 82.5 %collective-permute-start.1 = (f32[8,32,64]{2,1,0:T(8,128)S(1)}, f32[8,32,64]{2,1,0:T(8,128)S(1)}, u32[]{:S(2)}, u32[]{:S(2)}) collective-permute-start(f32[8,32,64]{2,1,0:T(8,128)S(1)} %bitcast.73), channel_id=1, source_target_pairs={{8,0},{16,8},{24,16},{32,24},{40,32},{48,40},{56,48},{64,56},{72,6... | collective-permute-start | bytes 196616 | tf_op jit(solution)/shard_map/ppermute | solution.py:21
  40.4 77.4 %copy-start.8 = (s32[1020,4]{0,1:T(4,128)S(1)}, s32[1020,4]{0,1:T(4,128)}, u32[]{:S(2)}) copy-start(s32[1020,4]{0,1:T(4,128)} %param.18) | copy-start | bytes 48964
  41.8 77.1 %copy-start.1 = (f32[8,32,256]{2,1,0:T(8,128)}, f32[8,32,256]{2,1,0:T(8,128)S(1)}, u32[]{:S(2)}) copy-start(f32[8,32,256]{2,1,0:T(8,128)S(1)} %copy.16.spread_ref) | copy-start | bytes 786436
  42.5 76.4 %collective-permute-start.5 = (f32[2,32,256]{2,1,0:T(8,128)}, f32[2,32,256]{2,1,0:T(8,128)S(1)}, u32[]{:S(2)}, u32[]{:S(2)}) collective-permute-start(f32[2,32,256]{2,1,0:T(8,128)} %get-tuple-element.5), channel_id=1, source_target_pairs={{1,0},{2,1},{3,2},{4,3},{5,4},{6,5},{7,6},{8,7},{9,8},{10,9},{11,1... | collective-permute-start | bytes 196616 | tf_op jit(solution)/shard_map/ppermute | solution.py:21
  49.5 69.4 %copy-start.6 = (f32[6,32,64]{2,1,0:T(8,128)}, f32[6,32,64]{2,1,0:T(8,128)S(1)}, u32[]{:S(2)}) copy-start(f32[6,32,64]{2,1,0:T(8,128)S(1)} %collective-permute-done.3) | copy-start | bytes 147460
  49.5 69.4 %collective-permute-start.4 = (f32[2,32,256]{2,1,0:T(8,128)}, f32[2,32,256]{2,1,0:T(8,128)}, u32[]{:S(2)}, u32[]{:S(2)}) collective-permute-start(f32[2,32,256]{2,1,0:T(8,128)} %get-tuple-element.6), channel_id=1, source_target_pairs={{0,1},{1,2},{2,3},{3,4},{4,5},{5,6},{6,7},{7,8},{8,9},{9,10},{10,1... | collective-permute-start | bytes 196616 | tf_op jit(solution)/shard_map/ppermute | solution.py:20
  118.8 0.6 copy-start.4
  118.8 0.7 copy-start.5
  118.9 0.7 copy-start.7

commit v4 on v3

--- a/solution.py
+++ b/solution.py
@@ -61,7 +61,7 @@
                 out_ref, p5, p6, p7, p8, p9, ext2_ref, e3, e4, *, starts, k, r, leaves, width, levels,
                 reach):
     def dot(a, b):
-        return jnp.dot(a, b, precision=highest, preferred_element_type=jnp.float32)
+        return jnp.dot(a, b, precision=lax.Precision.HIGH, preferred_element_type=jnp.float32)
 
     def halve_rows(x, n, height):
         v = x.reshape(n // 2, 2 * k, r)

time: 138 us -> 135 us (0.978)
  Pallas kernels: 17.9 us -> 15 us
    pallas_call x1, Pallas kernels: 17.9 us -> 15 us  [local(): pl.pallas_call(functools.partial(tree_kernel, starts=starts, k=k, r=r, le...]
  transfers between devices with their start and end apart: 6 -> 6, of which waited for: 0 -> 0; matrix products, arithmetic and copies ran while one was open for 7% -> 8% of each run, Pallas kernels for 0% -> 0%
where the time goes in v4:
time: 135 us
  blocking collectives  88.9 us (66%)
  starting transfers between devices  17.2 us (13%)
  Pallas kernels  15 us (11%)
  matrix products  8.42 us (6%)
  local copies, waits for them, and re-layouts  3.41 us (3%)
  other arithmetic  1.38 us (1%)
    all_gather x1, blocking collectives, local(): gathered = lax.all_gather(up_levels[-1][0], 'yz', axis=0, tiled=False)  65.2 us
    all_gather x1, blocking collectives, local(): grp = lax.all_gather(a2[0], GROUP, axis=0, tiled=False)  23.7 us
    pallas_call x1, Pallas kernels, local(): pl.pallas_call(functools.partial(tree_kernel, starts=starts, k=k, r=r, le...  15 us
    ppermute x3, starting transfers between devices, padded(): before = lax.ppermute(shard[length - width:], axis, up)  9.45 us
    ppermute x3, starting transfers between devices, padded(): after = lax.ppermute(shard[:width], axis, down)  7.75 us
    dot_general x5, matrix products, halve(): return jnp.einsum('bjkr,jrs->bks', paired, transfer, precision=highest)  5.41 us
  transfers between devices with their start and end apart: 6, of which 0 were waited for; matrix products, arithmetic and copies ran while one was open for 8% of the time, Pallas kernels for 0%

profile of v4, /device:TPU:6, one launch (start us, length us, event | category | flops | bytes accessed | tf_op | source)
XLA Modules:
  0.0 134.5 jit_solution(11493506271780963326)
XLA Ops:
  0.0 1.2 fusion.2
  1.2 1.1 convolution_bitcast_fusion.3
  2.4 2.7 %collective-permute-start.3 = (f32[6,32,64]{2,1,0:T(8,128)S(1)}, f32[6,32,64]{2,1,0:T(8,128)S(1)}, u32[]{:S(2)}, u32[]{:S(2)}) collective-permute-start(f32[6,32,64]{2,1,0:T(8,128)S(1)} %pad_maximum_fusion), channel_id=1, source_target_pairs={{1,0},{2,1},{3,2},{4,3},{5,4},{6,5},{7,6},{8,7},{9,8},{10,9},{11,1... | collective-permute-start | bytes 147464 | tf_op jit(solution)/shard_map/ppermute | solution.py:21
  5.1 4.0 %collective-permute-start.2 = (f32[6,32,64]{2,1,0:T(8,128)S(1)}, f32[6,32,64]{2,1,0:T(8,128)}, u32[]{:S(2)}, u32[]{:S(2)}) collective-permute-start(f32[6,32,64]{2,1,0:T(8,128)S(1)} %pad_maximum_fusion), channel_id=1, source_target_pairs={{0,1},{1,2},{2,3},{3,4},{4,5},{5,6},{6,7},{7,8},{8,9},{9,10},{10,1... | collective-permute-start | bytes 147464 | tf_op jit(solution)/shard_map/ppermute | solution.py:20
  9.2 1.1 convolution_bitcast_fusion.5
  10.2 23.7 %all-gather.gown_ref = f32[256,64]{1,0:T(8,128)S(1)} all-gather(f32[32,64]{1,0:T(8,128)S(1)} %convolution_bitcast_fusion.5), channel_id=2, replica_groups=mesh['yz'=64,'core'=2,'sub'=4] {'core','sub'}, dimensions={0}, use_global_device_ids=true | all-gather | bytes 73728 | tf_op jit(solution)/shard_map/all_gather | solution.py:190
  33.9 2.4 %collective-permute-start = (f32[8,32,64]{2,1,0:T(8,128)S(1)}, f32[8,32,64]{2,1,0:T(8,128)S(1)}, u32[]{:S(2)}, u32[]{:S(2)}) collective-permute-start(f32[8,32,64]{2,1,0:T(8,128)S(1)} %bitcast.72), channel_id=1, source_target_pairs={{0,8},{8,16},{16,24},{24,32},{32,40},{40,48},{48,56},{56,64},{64,7... | collective-permute-start | bytes 196616 | tf_op jit(solution)/shard_map/ppermute | solution.py:20
  36.3 1.3 collective-permute-start.1
  37.6 0.9 reshape.81
  38.5 0.7 broadcast_compare_fusion
  39.2 0.7 broadcast_subtract_fusion
  39.9 0.5 fusion.10
  40.4 1.3 convolution_bitcast_fusion
  41.7 0.1 copy.16.spread_ref
  41.8 0.7 fusion.22
  42.5 3.7 %collective-permute-start.5 = (f32[2,32,256]{2,1,0:T(8,128)}, f32[2,32,256]{2,1,0:T(8,128)S(1)}, u32[]{:S(2)}, u32[]{:S(2)}) collective-permute-start(f32[2,32,256]{2,1,0:T(8,128)} %get-tuple-element.5), channel_id=1, source_target_pairs={{1,0},{2,1},{3,2},{4,3},{5,4},{6,5},{7,6},{8,7},{9,8},{10,9},{11,1... | collective-permute-start | bytes 196616 | tf_op jit(solution)/shard_map/ppermute | solution.py:21
  46.2 1.1 convolution_bitcast_fusion.1
  47.4 1.1 convolution_bitcast_fusion.2
  48.4 1.1 convolution_bitcast_fusion.4
  49.5 0.0 collective-permute-done.3
  49.5 3.0 %collective-permute-start.4 = (f32[2,32,256]{2,1,0:T(8,128)}, f32[2,32,256]{2,1,0:T(8,128)}, u32[]{:S(2)}, u32[]{:S(2)}) collective-permute-start(f32[2,32,256]{2,1,0:T(8,128)} %get-tuple-element.6), channel_id=1, source_target_pairs={{0,1},{1,2},{2,3},{3,4},{4,5},{5,6},{6,7},{7,8},{8,9},{9,10},{10,1... | collective-permute-start | bytes 196616 | tf_op jit(solution)/shard_map/ppermute | solution.py:20
  52.6 65.2 %all-gather.1.top5_ref = f32[2048,64]{1,0:T(8,128)} all-gather(f32[32,64]{1,0:T(8,128)S(1)} %convolution_bitcast_fusion.4), channel_id=3, replica_groups=mesh['yz'=64,'core'=2,'sub'=4] {'yz'}, dimensions={0}, use_global_device_ids=true | all-gather | bytes 532480 | tf_op jit(solution)/shard_map/all_gather | solution.py:215
  117.8 1.1 copy.15.ftop_ref
  118.8 0.0 collective-permute-done.2
  118.8 0.0 collective-permute-done
  118.8 0.0 collective-permute-done.1
  118.9 0.0 collective-permute-done.5.ra_ref
  118.9 0.0 collective-permute-done.4.rb_ref
  118.9 0.6 copy-done.4
  119.5 0.0 copy-done.5
  119.5 0.0 copy-done.7
  119.6 15.0 %shard_map.109 = f32[32,1024]{1,0:T(8,128)} custom-call(s32[1]{0:T(128)} %bitcast.dev_ref, s32[1020,4]{1,0:T(8,128)} %copy.15.ftop_ref, s32[4,4]{1,0:T(4,128)} %fleaf_ref.1, s32[2,4]{1,0:T(2,128)} %fpair_ref.1, f32[2048,64]{1,0:T(8,128)} %all-gather.1.top5_ref, f32[256,64]{1,0:T(8,128)} %bitcast.79, f32[256,64]{1,0:T(8,128)} %copy-done.2, ...), custom_call_target="tpu_custom_call" | custom-call | tf_op jit(solution)/shard_map/pallas_call | solution.py:222
  (16 shorter events, 0.0 us)
Async XLA Ops:
  0.0 39.9 %copy-start = (bf16[4,5,256,256]{3,2,1,0:T(8,128)(2,1)S(1)}, bf16[4,5,256,256]{3,2,1,0:T(8,128)(2,1)}, u32[]{:S(2)}) copy-start(bf16[4,5,256,256]{3,2,1,0:T(8,128)(2,1)} %param.14) | copy-start | bytes 7864324
  2.4 39.4 %copy-start.3 = (f32[6,32,64]{2,1,0:T(8,128)}, f32[6,32,64]{2,1,0:T(8,128)S(1)}, u32[]{:S(2)}) copy-start(f32[6,32,64]{2,1,0:T(8,128)S(1)} %pad_maximum_fusion) | copy-start | bytes 147460
  2.4 47.1 %collective-permute-start.3 = (f32[6,32,64]{2,1,0:T(8,128)S(1)}, f32[6,32,64]{2,1,0:T(8,128)S(1)}, u32[]{:S(2)}, u32[]{:S(2)}) collective-permute-start(f32[6,32,64]{2,1,0:T(8,128)S(1)} %pad_maximum_fusion), channel_id=1, source_target_pairs={{1,0},{2,1},{3,2},{4,3},{5,4},{6,5},{7,6},{8,7},{9,8},{10,9},{11,1... | collective-permute-start | bytes 147464 | tf_op jit(solution)/shard_map/ppermute | solution.py:21
  5.1 113.7 %collective-permute-start.2 = (f32[6,32,64]{2,1,0:T(8,128)S(1)}, f32[6,32,64]{2,1,0:T(8,128)}, u32[]{:S(2)}, u32[]{:S(2)}) collective-permute-start(f32[6,32,64]{2,1,0:T(8,128)S(1)} %pad_maximum_fusion), channel_id=1, source_target_pairs={{0,1},{1,2},{2,3},{3,4},{4,5},{5,6},{6,7},{7,8},{8,9},{9,10},{10,1... | collective-permute-start | bytes 147464 | tf_op jit(solution)/shard_map/ppermute | solution.py:20
  33.9 12.3 %copy-start.2 = (f32[256,64]{1,0:T(8,128)}, f32[256,64]{1,0:T(8,128)S(1)}, u32[]{:S(2)}) copy-start(f32[256,64]{1,0:T(8,128)S(1)} %all-gather.gown_ref) | copy-start | bytes 196612
  33.9 84.9 %collective-permute-start = (f32[8,32,64]{2,1,0:T(8,128)S(1)}, f32[8,32,64]{2,1,0:T(8,128)S(1)}, u32[]{:S(2)}, u32[]{:S(2)}) collective-permute-start(f32[8,32,64]{2,1,0:T(8,128)S(1)} %bitcast.72), channel_id=1, source_target_pairs={{0,8},{8,16},{16,24},{24,32},{32,40},{40,48},{48,56},{56,64},{64,7... | collective-permute-start | bytes 196616 | tf_op jit(solution)/shard_map/ppermute | solution.py:20
  36.3 82.5 %collective-permute-start.1 = (f32[8,32,64]{2,1,0:T(8,128)S(1)}, f32[8,32,64]{2,1,0:T(8,128)S(1)}, u32[]{:S(2)}, u32[]{:S(2)}) collective-permute-start(f32[8,32,64]{2,1,0:T(8,128)S(1)} %bitcast.73), channel_id=1, source_target_pairs={{8,0},{16,8},{24,16},{32,24},{40,32},{48,40},{56,48},{64,56},{72,6... | collective-permute-start | bytes 196616 | tf_op jit(solution)/shard_map/ppermute | solution.py:21
  40.4 77.4 %copy-start.8 = (s32[1020,4]{0,1:T(4,128)S(1)}, s32[1020,4]{0,1:T(4,128)}, u32[]{:S(2)}) copy-start(s32[1020,4]{0,1:T(4,128)} %param.18) | copy-start | bytes 48964
  41.8 77.1 %copy-start.1 = (f32[8,32,256]{2,1,0:T(8,128)}, f32[8,32,256]{2,1,0:T(8,128)S(1)}, u32[]{:S(2)}) copy-start(f32[8,32,256]{2,1,0:T(8,128)S(1)} %copy.16.spread_ref) | copy-start | bytes 786436
  42.5 76.4 %collective-permute-start.5 = (f32[2,32,256]{2,1,0:T(8,128)}, f32[2,32,256]{2,1,0:T(8,128)S(1)}, u32[]{:S(2)}, u32[]{:S(2)}) collective-permute-start(f32[2,32,256]{2,1,0:T(8,128)} %get-tuple-element.5), channel_id=1, source_target_pairs={{1,0},{2,1},{3,2},{4,3},{5,4},{6,5},{7,6},{8,7},{9,8},{10,9},{11,1... | collective-permute-start | bytes 196616 | tf_op jit(solution)/shard_map/ppermute | solution.py:21
  49.5 69.4 %copy-start.6 = (f32[6,32,64]{2,1,0:T(8,128)}, f32[6,32,64]{2,1,0:T(8,128)S(1)}, u32[]{:S(2)}) copy-start(f32[6,32,64]{2,1,0:T(8,128)S(1)} %collective-permute-done.3) | copy-start | bytes 147460
  49.5 69.4 %collective-permute-start.4 = (f32[2,32,256]{2,1,0:T(8,128)}, f32[2,32,256]{2,1,0:T(8,128)}, u32[]{:S(2)}, u32[]{:S(2)}) collective-permute-start(f32[2,32,256]{2,1,0:T(8,128)} %get-tuple-element.6), channel_id=1, source_target_pairs={{0,1},{1,2},{2,3},{3,4},{4,5},{5,6},{6,7},{7,8},{8,9},{9,10},{10,1... | collective-permute-start | bytes 196616 | tf_op jit(solution)/shard_map/ppermute | solution.py:20
  118.8 0.6 copy-start.4
  118.8 0.7 copy-start.5
  118.9 0.7 copy-start.7
